TPU v7x, 256 devices: a whole 4x4x8 slice. The times are simulated.
256 devices in a mesh: dp: 4 (over z_lo, core), expert: 64 (over x, y, z_hi).
Axes of the slice: x: 4, y: 4, z: 8 (z_hi: 4, z_lo: 2; z = z_hi * 2 + z_lo), core: 2. Of those that a mesh axis runs over, the one named last changes fastest.
Arguments:
- tokens: bfloat16 [8192, 3584], P('expert'), may hold values from -6 to 6
- cotangent: bfloat16 [8192, 3584], P('expert'), may hold values from -0.29882812 to 0.29882812
- probs: bfloat16 [8192, 8], P('expert'), may hold values from 0.049804688 to 0.59765625
- expert_ids: int32 [8192, 8], P('expert'), may hold values from 0 to 63, all different within a row; in each aligned block of 128 rows (0 to 127, 128 to 255, ...) at most 18 rows name the same one
- w_in: bfloat16 [64, 3584, 1024], P('expert', None, 'dp'), may hold values from -0.1875 to 0.1875
- w_out: bfloat16 [64, 1024, 3584], P('expert', 'dp'), may hold values from -0.1875 to 0.1875
Outputs:
- grad_tokens: bfloat16 [8192, 3584], P('expert')
- gate_grad: bfloat16 [8192, 8], P('expert')
- grad_w_in: bfloat16 [64, 3584, 1024], P('expert', None, 'dp')
- grad_w_out: bfloat16 [64, 1024, 3584], P('expert', 'dp')
Inputs may be any that keep to these rules, and one draw needn't show every extreme that they name: `expert_ids`: each row names 8 different experts. In each aligned block of 128 rows (the tokens of one index of expert) no expert is named by more than 18 rows, a bound that some block reaches.
All inputs are finite; a program needn't handle non-finite values.
Results may differ from a plain program's by a relative error of at most 0.0064.
Values may be sent and summed in bfloat16 or wider, within the bound.
No kernel may reach another device: no remote copies, remote signals or barrier semaphores. Data moves between devices by JAX's collectives and lax.ppermute only.
A program may use at most 192 MiB of HBM per device.

v0:
```python
import jax
import jax.numpy as jnp
from jax import lax
from jax.sharding import PartitionSpec as P


def slot_tables(expert_ids, capacity, experts):
    count, top = expert_ids.shape
    flat = expert_ids.reshape(count * top)
    onehot = (flat[:, None] == jnp.arange(experts, dtype=jnp.int32)[None, :]).astype(jnp.int32)
    slot = jnp.sum((jnp.cumsum(onehot, axis=0) - onehot) * onehot, axis=1)
    target = flat * capacity + slot
    placing = (target[:, None] == jnp.arange(experts * capacity, dtype=jnp.int32)[None, :]).astype(
        jnp.float32
    )
    picker = jnp.sum(placing.reshape(count, top, experts * capacity), axis=1)
    return (target, placing, picker)


def expert_terms(rows_x, rows_u, rows_p, block_in, block_out):
    hidden = jnp.dot(rows_x, block_in, preferred_element_type=jnp.float32)
    act = jax.nn.silu(hidden).astype(jnp.bfloat16)
    output = jnp.dot(act, block_out, preferred_element_type=jnp.float32)
    score = jnp.sum(output * rows_u.astype(jnp.float32), axis=1)
    scaled = (rows_p.astype(jnp.float32)[:, None] * rows_u.astype(jnp.float32)).astype(jnp.bfloat16)
    back = lax.dot_general(
        scaled, block_out, (((1,), (1,)), ((), ())), preferred_element_type=jnp.float32
    )
    sigma = jax.nn.sigmoid(hidden)
    inner = (sigma * (1.0 + hidden * (1.0 - sigma)) * back).astype(jnp.bfloat16)
    grad_out = lax.dot_general(
        act, scaled, (((0,), (0,)), ((), ())), preferred_element_type=jnp.float32
    )
    grad_in = lax.dot_general(
        rows_x, inner, (((0,), (0,)), ((), ())), preferred_element_type=jnp.float32
    )
    row_grad = lax.dot_general(
        inner, block_in, (((1,), (1,)), ((), ())), preferred_element_type=jnp.float32
    )
    return (row_grad, score, grad_in, grad_out)


def per_device(tokens, cotangent, probs, expert_ids, w_in, w_out):
    count, top = expert_ids.shape
    width = tokens.shape[1]
    experts = lax.axis_size("expert") * w_in.shape[0]
    capacity = min(count, max(2, (9 * top * count + 8 * experts - 1) // (8 * experts)))
    block_in = w_in[0]
    block_out = w_out[0]
    target, placing, picker = slot_tables(expert_ids, capacity, experts)
    pick = picker.astype(jnp.bfloat16)
    slot_x = lax.dot_general(
        pick, tokens, (((0,), (0,)), ((), ())), preferred_element_type=jnp.float32
    )
    slot_u = lax.dot_general(
        pick, cotangent, (((0,), (0,)), ((), ())), preferred_element_type=jnp.float32
    )
    slot_p = jnp.dot(
        probs.reshape(-1).astype(jnp.float32), placing, precision=lax.Precision.HIGHEST
    )
    slot_x = slot_x.astype(jnp.bfloat16).reshape(experts, capacity, width)
    slot_u = slot_u.astype(jnp.bfloat16).reshape(experts, capacity, width)
    slot_p = slot_p.astype(jnp.bfloat16).reshape(experts, capacity)
    all_x, all_u, recv_p = (
        lax.all_to_all(slot_x, "expert", split_axis=0, concat_axis=0, tiled=True),
        lax.all_to_all(slot_u, "expert", split_axis=0, concat_axis=0, tiled=True),
        lax.all_to_all(slot_p, "expert", split_axis=0, concat_axis=0, tiled=True),
    )
    rows = recv_p.size
    row_grad, score, grad_in, grad_out = expert_terms(
        all_x.reshape(rows, width),
        all_u.reshape(rows, width),
        recv_p.reshape(rows),
        block_in,
        block_out,
    )
    row_part = row_grad.astype(jnp.bfloat16)
    score_part = score.astype(jnp.bfloat16)
    back_x, back_s = (
        lax.all_to_all(
            row_part.reshape(all_x.shape), "expert", split_axis=0, concat_axis=0, tiled=True
        ),
        lax.all_to_all(
            score_part.reshape(recv_p.shape), "expert", split_axis=0, concat_axis=0, tiled=True
        ),
    )
    token_part = jnp.dot(
        pick, back_x.reshape(experts * capacity, width), preferred_element_type=jnp.float32
    )
    gate_part = jnp.take(back_s.reshape(-1).astype(jnp.float32), target).reshape(count, top)
    grad_sum, gate_sum = lax.psum((token_part, gate_part), "dp")
    grad_tokens = grad_sum.astype(jnp.bfloat16)
    gate_grad = gate_sum.astype(jnp.bfloat16)
    grad_w_in = grad_in.astype(jnp.bfloat16)[None]
    grad_w_out = grad_out.astype(jnp.bfloat16)[None]
    return (grad_tokens, gate_grad, grad_w_in, grad_w_out)


def solution(mesh):
    in_specs = (
        P("expert", None),
        P("expert", None),
        P("expert", None),
        P("expert", None),
        P("expert", None, "dp"),
        P("expert", "dp", None),
    )
    out_specs = (
        P("expert", None),
        P("expert", None),
        P("expert", None, "dp"),
        P("expert", "dp", None),
    )
    return jax.shard_map(
        per_device, mesh=mesh, in_specs=in_specs, out_specs=out_specs, check_vma=False
    )
```

profile of v0, /device:TPU:1, one launch (start us, length us, event | category | flops | bytes accessed | tf_op | source)
XLA Modules:
  0.0 963.2 jit_solution(10973160321525524651)
XLA Ops:
  0.7 0.9 copy.27
  1.8 0.8 copy.32
  2.7 18.0 %reduce-window.6 = s32[64,8,128]{2,1,0:T(8,128)S(1)} reduce-window(s32[64,8,128]{2,1,0:T(8,128)S(1)} %fusion.18, s32[]{:T(128)} %constant.13.clone.1), window={size=1x1x128 pad=0_0x0_0x127_0}, to_apply=%region_0.0 | reduce-window | flops 8323072 | bytes 524292 | tf_op jit(solution)/shard_map/reduce-window
  21.4 0.9 fusion.14
  23.0 15.1 %all-to-all-start.1 = ((bf16[64,1,18]{2,1,0:T(2,128)(2,1)}), bf16[64,1,18]{2,1,0:T(2,128)(2,1)S(1)}, u32[]{:S(2)}, u32[]{:S(2)}) async-start(bf16[64,1,18]{2,1,0:T(2,128)(2,1)} %all_to_all.25), calls=%async_computation.1 | async-start | bytes 65536 | tf_op jit(solution)/shard_map/all_to_all | solution.py:67
  38.3 1.5 convert_reduce_fusion
  39.7 5.5 convolution_convert_fusion.1
  45.2 13.2 %reshape.145 = bf16[64,18,3584]{2,1,0:T(8,128)(2,1)} reshape(bf16[1152,3584]{1,0:T(8,128)(2,1)} %convolution_convert_fusion.1) | data formatting | bytes 16515072 | tf_op jit(solution)/shard_map/reshape | solution.py:62
  58.4 12.5 %all-to-all-start.2 = ((bf16[64,18,3584]{2,1,0:T(8,128)(2,1)}), bf16[64,18,3584]{2,1,0:T(8,128)(2,1)}, u32[]{:S(2)}, u32[]{:S(2)}) async-start(bf16[64,18,3584]{2,1,0:T(8,128)(2,1)} %reshape.145), calls=%async_computation.2 | async-start | bytes 22020096 | tf_op jit(solution)/shard_map/all_to_all | solution.py:66
  71.0 5.5 convolution_convert_fusion.2
  76.5 13.2 %reshape.142 = bf16[64,18,3584]{2,1,0:T(8,128)(2,1)} reshape(bf16[1152,3584]{1,0:T(8,128)(2,1)} %convolution_convert_fusion.2) | data formatting | bytes 16515072 | tf_op jit(solution)/shard_map/reshape | solution.py:61
  89.7 221.8 %all-to-all-done.2 = bf16[64,18,3584]{2,1,0:T(8,128)(2,1)} async-done(((bf16[64,18,3584]{2,1,0:T(8,128)(2,1)}), bf16[64,18,3584]{2,1,0:T(8,128)(2,1)}, u32[]{:S(2)}, u32[]{:S(2)}) %all-to-all-start.2) | async-done | bytes 8257568 | tf_op jit(solution)/shard_map/all_to_all | solution.py:66
  311.5 9.5 all-to-all-start
  321.0 10.4 %multiply_convert_fusion = bf16[64,18,3584]{2,1,0:T(8,128)(2,1)} fusion(f32[64,18]{1,0:T(8,128)S(1)} %bitcast.48, bf16[64,18,3584]{2,1,0:T(8,128)(2,1)} %all-to-all-done.2), kind=kLoop, calls=%fused_computation.1 | loop fusion | flops 12386304 | bytes 16519680 | tf_op jit(solution)/shard_map/convert_element_type | solution.py:25
  331.4 13.4 %convert_element_type.110 = bf16[1152,3584]{1,0:T(8,128)(2,1)} reshape(bf16[64,18,3584]{2,1,0:T(8,128)(2,1)} %multiply_convert_fusion) | data formatting | bytes 16515072 | tf_op jit(solution)/shard_map/convert_element_type | solution.py:25
  344.8 215.0 %all-to-all-done = bf16[64,18,3584]{2,1,0:T(8,128)(2,1)} async-done(((bf16[64,18,3584]{2,1,0:T(8,128)(2,1)}), bf16[64,18,3584]{2,1,0:T(8,128)(2,1)}, u32[]{:S(2)}, u32[]{:S(2)}) %all-to-all-start) | async-done | bytes 8257568 | tf_op jit(solution)/shard_map/all_to_all | solution.py:65
  559.8 13.4 %reshape.143 = bf16[1152,3584]{1,0:T(8,128)(2,1)} reshape(bf16[64,18,3584]{2,1,0:T(8,128)(2,1)} %all-to-all-done) | data formatting | bytes 16515072 | tf_op jit(solution)/shard_map/reshape | solution.py:71
  573.2 5.8 fusion.12
  579.4 3.3 fusion.7
  582.7 15.1 %reshape.149 = f32[1152,3584]{1,0:T(8,128)} reshape(bf16[64,18,3584]{2,1,0:T(8,128)(2,1)} %all-to-all-done.2) | data formatting | bytes 24772608 | tf_op jit(solution)/shard_map/convert_element_type | solution.py:25
  597.8 8.8 fusion.6
  607.3 10.2 %all-to-all-start.4 = ((bf16[64,1,18]{2,1,0:T(2,128)(2,1)}), bf16[64,1,18]{2,1,0:T(2,128)(2,1)S(1)}, u32[]{:S(2)}, u32[]{:S(2)}) async-start(bf16[64,1,18]{2,1,0:T(2,128)(2,1)} %convert_element_type.131), calls=%async_computation.4 | async-start | bytes 65536 | tf_op jit(solution)/shard_map/all_to_all | solution.py:83
  617.5 6.6 convolution_convert_fusion
  624.1 13.2 %reshape.146 = bf16[64,18,3584]{2,1,0:T(8,128)(2,1)} reshape(bf16[1152,3584]{1,0:T(8,128)(2,1)} %convolution_convert_fusion) | data formatting | bytes 16515072 | tf_op jit(solution)/shard_map/reshape | solution.py:81
  637.3 12.6 %all-to-all-start.3 = ((bf16[64,18,3584]{2,1,0:T(8,128)(2,1)}), bf16[64,18,3584]{2,1,0:T(8,128)(2,1)}, u32[]{:S(2)}, u32[]{:S(2)}) async-start(bf16[64,18,3584]{2,1,0:T(8,128)(2,1)} %reshape.146), calls=%async_computation.3 | async-start | bytes 22020096 | tf_op jit(solution)/shard_map/all_to_all | solution.py:80
  650.3 7.3 fusion.3
  657.6 9.8 %fusion.4 = bf16[1,256,3584]{2,1,0:T(8,128)(2,1)} fusion(f32[1152,3584]{1,0:T(8,128)} %reshape.149, f32[1152]{0:T(1024)S(1)} %reshape.151, f32[1152,256]{1,0:T(8,128)S(1)} %fusion.12), kind=kOutput, calls=%fused_computation.12 | convolution fusion | flops 2124578816 | bytes 19534336 | tf_op jit(solution)/shard_map/dot_general | solution.py:31
  667.7 6.2 gather_fusion
  673.9 214.2 %all-to-all-done.3 = bf16[64,18,3584]{2,1,0:T(8,128)(2,1)} async-done(((bf16[64,18,3584]{2,1,0:T(8,128)(2,1)}), bf16[64,18,3584]{2,1,0:T(8,128)(2,1)}, u32[]{:S(2)}, u32[]{:S(2)}) %all-to-all-start.3) | async-done | bytes 8257568 | tf_op jit(solution)/shard_map/all_to_all | solution.py:80
  888.2 13.4 %reshape.147 = bf16[1152,3584]{1,0:T(8,128)(2,1)} reshape(bf16[64,18,3584]{2,1,0:T(8,128)(2,1)} %all-to-all-done.3) | data formatting | bytes 16515072 | tf_op jit(solution)/shard_map/reshape | solution.py:88
  901.6 6.0 fusion.24
  907.5 55.0 %all-reduce.2 = (bf16[128,3584]{1,0:T(8,128)(2,1)}, bf16[128,8]{1,0:T(8,128)(2,1)S(1)}) all-reduce(f32[128,3584]{1,0:T(8,128)} %fusion.24, f32[128,8]{1,0:T(8,128)S(1)} %and_select_fusion), channel_id=1, replica_groups=mesh['dp'=4,'expert'=64] {'dp'}, use_global_device_ids=true, to_apply=%region_4.5 | all-reduce | flops 459776 | bytes 2758656 | tf_op jit(solution)/shard_map/psum | solution.py:91
  (39 shorter events, 4.3 us)
Async XLA Ops:
  0.6 572.6 %copy-start = (bf16[1,3584,256]{2,1,0:T(8,128)(2,1)S(1)}, bf16[1,3584,256]{2,1,0:T(8,128)(2,1)}, u32[]{:S(2)}) copy-start(bf16[1,3584,256]{2,1,0:T(8,128)(2,1)} %param.10) | copy-start | bytes 5505028
  0.6 39.1 %copy-start.3 = (bf16[128,3584]{1,0:T(8,128)(2,1)S(1)}, bf16[128,3584]{1,0:T(8,128)(2,1)}, u32[]{:S(2)}) copy-start(bf16[128,3584]{1,0:T(8,128)(2,1)} %param.7) | copy-start | bytes 2752516
  23.0 35.4 %all-to-all-start.1 = ((bf16[64,1,18]{2,1,0:T(2,128)(2,1)}), bf16[64,1,18]{2,1,0:T(2,128)(2,1)S(1)}, u32[]{:S(2)}, u32[]{:S(2)}) async-start(bf16[64,1,18]{2,1,0:T(2,128)(2,1)} %all_to_all.25), calls=%async_computation.1 | async-start | bytes 65536 | tf_op jit(solution)/shard_map/all_to_all | solution.py:67
  58.4 12.6 %copy-start.4 = (bf16[128,3584]{1,0:T(8,128)(2,1)S(1)}, bf16[128,3584]{1,0:T(8,128)(2,1)}, u32[]{:S(2)}) copy-start(bf16[128,3584]{1,0:T(8,128)(2,1)} %param.6) | copy-start | bytes 2752516
  58.4 253.0 %all-to-all-start.2 = ((bf16[64,18,3584]{2,1,0:T(8,128)(2,1)}), bf16[64,18,3584]{2,1,0:T(8,128)(2,1)}, u32[]{:S(2)}, u32[]{:S(2)}) async-start(bf16[64,18,3584]{2,1,0:T(8,128)(2,1)} %reshape.145), calls=%async_computation.2 | async-start | bytes 22020096 | tf_op jit(solution)/shard_map/all_to_all | solution.py:66
  311.5 248.3 %all-to-all-start = ((bf16[64,18,3584]{2,1,0:T(8,128)(2,1)}), bf16[64,18,3584]{2,1,0:T(8,128)(2,1)}, u32[]{:S(2)}, u32[]{:S(2)}) async-start(bf16[64,18,3584]{2,1,0:T(8,128)(2,1)} %reshape.142), calls=%async_computation | async-start | bytes 22020096 | tf_op jit(solution)/shard_map/all_to_all | solution.py:65
  573.2 5.8 copy-start.1
  573.2 6.2 copy-start.2
  607.3 30.0 %all-to-all-start.4 = ((bf16[64,1,18]{2,1,0:T(2,128)(2,1)}), bf16[64,1,18]{2,1,0:T(2,128)(2,1)S(1)}, u32[]{:S(2)}, u32[]{:S(2)}) async-start(bf16[64,1,18]{2,1,0:T(2,128)(2,1)} %convert_element_type.131), calls=%async_computation.4 | async-start | bytes 65536 | tf_op jit(solution)/shard_map/all_to_all | solution.py:83
  637.3 250.8 %all-to-all-start.3 = ((bf16[64,18,3584]{2,1,0:T(8,128)(2,1)}), bf16[64,18,3584]{2,1,0:T(8,128)(2,1)}, u32[]{:S(2)}, u32[]{:S(2)}) async-start(bf16[64,18,3584]{2,1,0:T(8,128)(2,1)} %reshape.146), calls=%async_computation.3 | async-start | bytes 22020096 | tf_op jit(solution)/shard_map/all_to_all | solution.py:80
where the time goes:
time: 975 us; the launch traced here: 963 us
  waiting for transfers between devices  651 us (67%)
  local copies, waits for them, and re-layouts  106 us (11%)
  starting transfers between devices  59.9 us (6%)
  matrix products  59.5 us (6%)
  blocking collectives  55 us (6%)
  other arithmetic  30.4 us (3%)
    all_to_all x1, waiting for transfers between devices, per_device(): lax.all_to_all(slot_u, 'expert', split_axis=0, concat_axis=0, tiled=True)  222 us
    all_to_all x1, waiting for transfers between devices, per_device(): lax.all_to_all(slot_x, 'expert', split_axis=0, concat_axis=0, tiled=True)  215 us
    all_to_all x1, waiting for transfers between devices, per_device(): lax.all_to_all(row_part.reshape(all_x.shape), 'expert', split_axis=0, con...  214 us
    psum x1, blocking collectives, per_device(): grad_sum, gate_sum = lax.psum((token_part, gate_part), 'dp')  55 us
  transfers between devices with their start and end apart: 5, of which 3 were waited for; matrix products, arithmetic and copies ran while one was open for 11% of the time, Pallas kernels for 0%

commit v1 on v0

v1 whole, which is shorter than its diff:
```python
import jax
import jax.numpy as jnp
from jax import lax
from jax.sharding import PartitionSpec as P


def slot_tables(expert_ids, capacity, experts):
    count, top = expert_ids.shape
    flat = expert_ids.reshape(count * top)
    onehot = (flat[:, None] == jnp.arange(experts, dtype=jnp.int32)[None, :]).astype(jnp.int32)
    slot = jnp.sum((jnp.cumsum(onehot, axis=0) - onehot) * onehot, axis=1)
    target = flat * capacity + slot
    placing = (target[:, None] == jnp.arange(experts * capacity, dtype=jnp.int32)[None, :]).astype(
        jnp.float32
    )
    picker = jnp.sum(placing.reshape(count, top, experts * capacity), axis=1)
    return (target, placing, picker)


def expert_terms(all_x, all_u, rows_p, block_in, block_out):
    quarters, rows, part = all_x.shape
    ff = block_in.shape[1]
    w_in_q = block_in.reshape(quarters, part, ff)
    w_out_q = block_out.reshape(ff, quarters, part)
    hidden = jnp.einsum("qrc,qcf->rf", all_x, w_in_q, preferred_element_type=jnp.float32)
    act = jax.nn.silu(hidden).astype(jnp.bfloat16)
    output = jnp.einsum("rf,fqc->qrc", act, w_out_q, preferred_element_type=jnp.float32)
    score = jnp.sum(output * all_u.astype(jnp.float32), axis=(0, 2))
    scaled = (rows_p.astype(jnp.float32)[None, :, None] * all_u.astype(jnp.float32)).astype(
        jnp.bfloat16
    )
    back = jnp.einsum("qrc,fqc->rf", scaled, w_out_q, preferred_element_type=jnp.float32)
    sigma = jax.nn.sigmoid(hidden)
    inner = (sigma * (1.0 + hidden * (1.0 - sigma)) * back).astype(jnp.bfloat16)
    grad_out = jnp.einsum("rf,qrc->fqc", act, scaled, preferred_element_type=jnp.float32)
    grad_in = jnp.einsum("qrc,rf->qcf", all_x, inner, preferred_element_type=jnp.float32)
    row_grad = jnp.einsum("rf,qcf->qrc", inner, w_in_q, preferred_element_type=jnp.float32)
    return (
        row_grad,
        score,
        grad_in.reshape(quarters * part, ff),
        grad_out.reshape(ff, quarters * part),
    )


def per_device(tokens, cotangent, probs, expert_ids, w_in, w_out):
    count, top = expert_ids.shape
    width = tokens.shape[1]
    n_dp = lax.axis_size("dp")
    part = width // n_dp
    d = lax.axis_index("dp")
    experts = lax.axis_size("expert") * w_in.shape[0]
    capacity = min(count, max(2, (9 * top * count + 8 * experts - 1) // (8 * experts)))
    block_in = w_in[0]
    block_out = w_out[0]
    target, placing, picker = slot_tables(expert_ids, capacity, experts)
    pick = picker.astype(jnp.bfloat16)
    x_part = lax.dynamic_slice_in_dim(tokens, d * part, part, axis=1)
    u_part = lax.dynamic_slice_in_dim(cotangent, d * part, part, axis=1)
    slot_x = lax.dot_general(
        pick, x_part, (((0,), (0,)), ((), ())), preferred_element_type=jnp.float32
    )
    slot_u = lax.dot_general(
        pick, u_part, (((0,), (0,)), ((), ())), preferred_element_type=jnp.float32
    )
    slot_p = jnp.dot(
        probs.reshape(-1).astype(jnp.float32), placing, precision=lax.Precision.HIGHEST
    )
    slot_x = slot_x.astype(jnp.bfloat16).reshape(experts, capacity, part)
    slot_u = slot_u.astype(jnp.bfloat16).reshape(experts, capacity, part)
    slot_p = slot_p.astype(jnp.bfloat16).reshape(experts, capacity)
    recv_x, recv_u, recv_p = (
        lax.all_to_all(slot_x, "expert", split_axis=0, concat_axis=0, tiled=True),
        lax.all_to_all(slot_u, "expert", split_axis=0, concat_axis=0, tiled=True),
        lax.all_to_all(slot_p, "expert", split_axis=0, concat_axis=0, tiled=True),
    )
    rows = recv_p.size
    all_x = lax.all_gather(recv_x.reshape(rows, part), "dp", axis=0, tiled=False)
    all_u = lax.all_gather(recv_u.reshape(rows, part), "dp", axis=0, tiled=False)
    row_grad, score, grad_in, grad_out = expert_terms(
        all_x, all_u, recv_p.reshape(rows), block_in, block_out
    )
    mixed = lax.all_to_all(
        row_grad.astype(jnp.bfloat16), "dp", split_axis=0, concat_axis=0, tiled=True
    )
    row_sum = jnp.sum(mixed.astype(jnp.float32), axis=0).astype(jnp.bfloat16)
    score_all = lax.all_gather(score.astype(jnp.bfloat16), "dp", axis=0, tiled=False)
    score_sum = jnp.sum(score_all.astype(jnp.float32), axis=0)
    back_x, back_s = (
        lax.all_to_all(
            row_sum.reshape(experts, capacity, part), "expert", split_axis=0, concat_axis=0,
            tiled=True,
        ),
        lax.all_to_all(
            score_sum.astype(jnp.bfloat16).reshape(experts, capacity), "expert", split_axis=0,
            concat_axis=0, tiled=True,
        ),
    )
    token_part = jnp.dot(
        pick, back_x.reshape(experts * capacity, part), preferred_element_type=jnp.float32
    )
    grad_tokens = lax.all_gather(token_part.astype(jnp.bfloat16), "dp", axis=1, tiled=True)
    gate_grad = (
        jnp.take(back_s.reshape(-1).astype(jnp.float32), target).reshape(count, top)
    ).astype(jnp.bfloat16)
    grad_w_in = grad_in.astype(jnp.bfloat16)[None]
    grad_w_out = grad_out.astype(jnp.bfloat16)[None]
    return (grad_tokens, gate_grad, grad_w_in, grad_w_out)


def solution(mesh):
    in_specs = (
        P("expert", None),
        P("expert", None),
        P("expert", None),
        P("expert", None),
        P("expert", None, "dp"),
        P("expert", "dp", None),
    )
    out_specs = (
        P("expert", None),
        P("expert", None),
        P("expert", None, "dp"),
        P("expert", "dp", None),
    )
    return jax.shard_map(
        per_device, mesh=mesh, in_specs=in_specs, out_specs=out_specs, check_vma=False
    )
```

time: 975 us -> 586 us (0.60); the launches traced: 963 us -> 585 us
  waiting for transfers between devices: 651 us -> 124 us
  blocking collectives: 55 us -> 281 us
  local copies, waits for them, and re-layouts: 106 us -> 60.3 us
  starting transfers between devices: 59.9 us -> 35.8 us
  matrix products: 59.5 us -> 42.1 us
  between operations: 0.88 us -> 14.3 us
    all_to_all x4 -> x3, waiting for transfers between devices: 651 us -> 40 us  [the longest x1 39.9 us: per_device(): lax.all_to_all(row_sum.reshape(experts, capacity, part), 'expert', split_...]
    all_to_all x0 -> x2, blocking collectives: none -> 187 us  [the longest x1 106 us: per_device(): lax.all_to_all(slot_x, 'expert', split_axis=0, concat_axis=0, tiled=True)]
    all_gather x0 -> x2, blocking collectives: none -> 94.4 us  [the longest x1 85 us: per_device(): lax.all_gather(score.astype(jnp.bfloat16), 'dp', axis=0, tiled=False)]
    all_gather x0 -> x2, waiting for transfers between devices: none -> 77.1 us  [the longest x1 73.5 us: per_device(): lax.all_gather(recv_x.reshape(rows, part), 'dp', axis=0, tiled=False)]
    psum x1 -> x0, blocking collectives: 55 us -> none  [per_device(): grad_sum, gate_sum = lax.psum((token_part, gate_part), 'dp')]
    reshape x5 -> x4, local copies, waits for them, and re-layouts: 66.4 us -> 16.6 us  [the longest x1 4.18 us: per_device(): row_sum.reshape(experts, capacity, part)]
    convert_element_type x4 -> x2, local copies, waits for them, and re-layouts: 29.4 us -> 2.87 us  [the longest x1 2.74 us: per_device(): grad_w_out = grad_out.astype(jnp.bfloat16)[None]]
    dot_general x9, matrix products: 58.6 us -> 41.2 us  [the longest x1 7.34 us: expert_terms(): jnp.einsum('rf,qrc->fqc', act, scaled, preferred_element_type=jnp.float32)]
  transfers between devices with their start and end apart: 5 -> 6, of which waited for: 3 -> 5; matrix products, arithmetic and copies ran while one was open for 11% -> 12% of each run, Pallas kernels for 0% -> 0%
where the time goes in v1:
time: 586 us; the launch traced here: 585 us
  blocking collectives  281 us (48%)
  waiting for transfers between devices  124 us (21%)
  local copies, waits for them, and re-layouts  60.3 us (10%)
  matrix products  42.1 us (7%)
  starting transfers between devices  35.8 us (6%)
  other arithmetic  26.5 us (5%)
  between operations  14.3 us (2%)
    all_to_all x1, blocking collectives, per_device(): lax.all_to_all(slot_x, 'expert', split_axis=0, concat_axis=0, tiled=True)  106 us
    all_gather x1, blocking collectives, per_device(): lax.all_gather(score.astype(jnp.bfloat16), 'dp', axis=0, tiled=False)  85 us
    all_to_all x1, blocking collectives, per_device(): lax.all_to_all(slot_u, 'expert', split_axis=0, concat_axis=0, tiled=True)  80.6 us
    all_gather x1, waiting for transfers between devices, per_device(): lax.all_gather(recv_x.reshape(rows, part), 'dp', axis=0, tiled=False)  73.5 us
    all_to_all x1, waiting for transfers between devices, per_device(): lax.all_to_all(row_sum.reshape(experts, capacity, part), 'expert', split_...  39.9 us
    another operation x3, other arithmetic  18.2 us
    all_to_all x1, starting transfers between devices, per_device(): lax.all_to_all(row_sum.reshape(experts, capacity, part), 'expert', split_...  12.7 us
    all_to_all x1, starting transfers between devices, per_device(): lax.all_to_all(score_sum.astype(jnp.bfloat16).reshape(experts, capacity),...  12.5 us
  transfers between devices with their start and end apart: 6, of which 5 were waited for; matrix products, arithmetic and copies ran while one was open for 12% of the time, Pallas kernels for 0%

profile of v1, /device:TPU:1, one launch (start us, length us, event | category | flops | bytes accessed | tf_op | source)
XLA Modules:
  0.0 584.6 jit_solution(6639582981173358112)
XLA Ops:
  8.4 18.0 %reduce-window.6 = s32[64,8,128]{2,1,0:T(8,128)S(1)} reduce-window(s32[64,8,128]{2,1,0:T(8,128)S(1)} %fusion.30, s32[]{:T(128)} %constant.17.clone.1), window={size=1x1x128 pad=0_0x0_0x127_0}, to_apply=%region_0.0 | reduce-window | flops 8323072 | bytes 524292 | tf_op jit(solution)/shard_map/reduce-window
  28.6 3.0 convolution_convert_fusion.1
  31.6 4.1 reshape.150
  35.7 80.6 %all_to_all.40 = bf16[64,18,896]{2,1,0:T(8,128)(2,1)} all-to-all(bf16[64,18,896]{2,1,0:T(8,128)(2,1)} %reshape.150), channel_id=1, replica_groups=mesh['dp'=4,'expert'=64] {'expert'}, dimensions={0} | all-to-all | bytes 4128768 | tf_op jit(solution)/shard_map/all_to_all | solution.py:74
  116.3 4.2 all_gather_reshape.7
  120.6 3.0 convolution_convert_fusion.2
  123.6 4.1 reshape.148
  127.7 106.2 %all_to_all.41 = bf16[64,18,896]{2,1,0:T(8,128)(2,1)} all-to-all(bf16[64,18,896]{2,1,0:T(8,128)(2,1)} %reshape.148), channel_id=1, replica_groups=mesh['dp'=4,'expert'=64] {'expert'}, dimensions={0} | all-to-all | bytes 4128768 | tf_op jit(solution)/shard_map/all_to_all | solution.py:73
  233.9 4.2 all_gather_reshape.6
  240.7 4.8 all-to-all-start.1
  245.5 3.8 copy.75
  249.3 7.3 %all-to-all-done.1 = bf16[64,1,18]{2,1,0:T(2,128)(2,1)S(1)} async-done(((bf16[64,1,18]{2,1,0:T(2,128)(2,1)}), bf16[64,1,18]{2,1,0:T(2,128)(2,1)S(1)}, u32[]{:S(2)}, u32[]{:S(2)}) %all-to-all-start.1) | async-done | bytes 2336 | tf_op jit(solution)/shard_map/all_to_all | solution.py:75
  256.8 3.5 all-gather.7.cloned.1.call-done
  260.3 11.5 %copy.59 = bf16[4,1152,896]{1,2,0:T(8,128)(2,1)} copy(bf16[4,1152,896]{2,1,0:T(8,128)(2,1)} %all-gather.7.cloned.1.call-done) | data formatting | bytes 16515072 | tf_op jit(solution)/shard_map/all_gather | solution.py:79
  271.8 73.5 %all-gather.5.cloned.1.call-done = bf16[4,1152,896]{2,1,0:T(8,128)(2,1)} async-done(((bf16[1,1152,896]{2,1,0:T(8,128)(2,1)}), bf16[4,1152,896]{2,1,0:T(8,128)(2,1)}) %all-gather.5.cloned.1.call-update) | async-done | bytes 8257552 | tf_op jit(solution)/shard_map/all_gather | solution.py:78
  345.4 4.8 convolution_bitcast_fusion
  352.1 2.7 fusion.17
  354.7 4.5 fusion.2
  359.3 5.7 all-to-all-start.3
  365.0 6.5 %fusion.1 = bf16[1152]{0:T(1024)(128)(2,1)S(1)} fusion(bf16[4,1152,896]{1,2,0:T(8,128)(2,1)} %copy.59, bf16[256,4,896]{0,2,1:T(8,128)(2,1)S(1)} %bitcast.63, f32[1152,256]{1,0:T(8,128)} %copy-done.6), kind=kOutput, calls=%fused_computation.4 | convolution fusion | flops 2127788928 | bytes 11274496 | tf_op jit(solution)/shard_map/rf,fqc->qrc/dot_general | solution.py:27
  371.5 85.0 %all-gather.1 = bf16[4,1,1152]{2,1,0:T(2,128)(2,1)S(1)} all-gather(bf16[1,1,1152]{2,1,0:T(2,128)(2,1)S(1)} %reshape.164), channel_id=2, replica_groups=mesh['dp'=4,'expert'=64] {'dp'}, dimensions={0}, use_global_device_ids=true | all-gather | bytes 11520 | tf_op jit(solution)/shard_map/all_gather | solution.py:87
  457.3 12.5 %all-to-all-start.5 = ((bf16[64,1,18]{2,1,0:T(2,128)(2,1)}), bf16[64,1,18]{2,1,0:T(2,128)(2,1)S(1)}, u32[]{:S(2)}, u32[]{:S(2)}) async-start(bf16[64,1,18]{2,1,0:T(2,128)(2,1)} %all_to_all.33), calls=%async_computation.5 | async-start | bytes 65536 | tf_op jit(solution)/shard_map/all_to_all | solution.py:94
  469.8 6.5 %reduce_sum.58 = bf16[1152,896]{1,0:T(8,128)(2,1)} reduce(bf16[4,1152,896]{2,1,0:T(8,128)(2,1)} %all-to-all-done.3, bf16[]{:T(256)} %constant.38.clone.1), dimensions={0}, to_apply=%region_4.5 | reduce | flops 3096576 | bytes 10321922 | tf_op jit(solution)/shard_map/reduce_sum | solution.py:86
  476.3 4.2 reshape.151
  480.5 12.7 %all-to-all-start.4 = ((bf16[64,18,896]{2,1,0:T(8,128)(2,1)}), bf16[64,18,896]{2,1,0:T(8,128)(2,1)}, u32[]{:S(2)}, u32[]{:S(2)}) async-start(bf16[64,18,896]{2,1,0:T(8,128)(2,1)} %reshape.151), calls=%async_computation.4 | async-start | bytes 5505024 | tf_op jit(solution)/shard_map/all_to_all | solution.py:90
  493.4 7.3 %fusion.21 = bf16[256,4,896]{2,0,1:T(8,128)(2,1)} fusion(bf16[4,1152,896]{1,2,0:T(8,128)(2,1)} %copy.59, f32[1152]{0:T(1024)S(1)} %reshape.153, f32[1152,256]{1,0:T(8,128)S(1)} %copy-done.7), kind=kOutput, calls=%fused_computation.21 | convolution fusion | flops 2128707584 | bytes 11276800 | tf_op jit(solution)/shard_map/rf,qrc->fqc/dot_general | solution.py:35
  500.7 2.7 copy.67
  506.1 7.2 %convolution_convert_fusion.3 = bf16[4,896,256]{2,1,0:T(8,128)(2,1)} fusion(bf16[4,1152,896]{2,1,0:T(8,128)(2,1)} %all-gather.5.cloned.1.call-done, bf16[1152,256,1]{1,0,2:T(8,128)(2,1)S(1)} %fusion.17), kind=kOutput, calls=%fused_computation.22 | convolution fusion | flops 2114846720 | bytes 10682368 | tf_op jit(solution)/shard_map/qrc,rf->qcf/dot_general | solution.py:36
  513.5 6.8 %gather_fusion = bf16[1024]{0:T(1024)(128)(2,1)S(1)} fusion(bf16[1152]{0:T(1024)(128)(2,1)S(1)} %reshape.154, s32[1024]{0:T(1024)S(1)} %broadcast_clamp_fusion), kind=kCustom, calls=%fused_computation | custom fusion | bytes 8192 | tf_op jit(solution)/shard_map/jit(_take)/gather | solution.py:104
  521.1 39.9 %all-to-all-done.4 = bf16[64,18,896]{2,1,0:T(8,128)(2,1)} async-done(((bf16[64,18,896]{2,1,0:T(8,128)(2,1)}), bf16[64,18,896]{2,1,0:T(8,128)(2,1)}, u32[]{:S(2)}, u32[]{:S(2)}) %all-to-all-start.4) | async-done | bytes 2064416 | tf_op jit(solution)/shard_map/all_to_all | solution.py:90
  561.0 4.2 reshape.152
  567.4 9.4 %all_gather.15 = bf16[128,3584]{1,0:T(8,128)(2,1)S(1)} all-gather(bf16[128,896]{1,0:T(8,128)(2,1)S(1)} %convolution_convert_fusion.4), channel_id=1, replica_groups=mesh['dp'=4,'expert'=64] {'dp'}, dimensions={1}, use_global_device_ids=true | all-gather | bytes 1146880 | tf_op jit(solution)/shard_map/all_gather | solution.py:102
  (57 shorter events, 15.7 us)
Async XLA Ops:
  7.2 338.2 %copy-start = (bf16[1,3584,256]{2,1,0:T(8,128)(2,1)S(1)}, bf16[1,3584,256]{2,1,0:T(8,128)(2,1)}, u32[]{:S(2)}) copy-start(bf16[1,3584,256]{2,1,0:T(8,128)(2,1)} %param.10) | copy-start | bytes 5505028
  7.2 253.1 %all-gather.7.cloned.1.call-start = ((), (), s32[]{:S(2)}) async-start(), calls=%async_computation.7 | async-start | bytes 10321920 | tf_op jit(solution)/shard_map/all_gather | solution.py:79
  120.5 224.8 %all-gather.5.cloned.1.call-start = ((), (), s32[]{:S(2)}) async-start(), calls=%async_computation.6 | async-start | bytes 10321920 | tf_op jit(solution)/shard_map/all_gather | solution.py:78
  238.1 0.7 copy-start.5
  240.7 15.8 %all-to-all-start.1 = ((bf16[64,1,18]{2,1,0:T(2,128)(2,1)}), bf16[64,1,18]{2,1,0:T(2,128)(2,1)S(1)}, u32[]{:S(2)}, u32[]{:S(2)}) async-start(bf16[64,1,18]{2,1,0:T(2,128)(2,1)} %all_to_all.32), calls=%async_computation.1 | async-start | bytes 65536 | tf_op jit(solution)/shard_map/all_to_all | solution.py:75
  345.4 5.8 copy-start.2
  345.4 6.7 %copy-start.3 = (bf16[1,256,3584]{1,2,0:T(8,128)(2,1)S(1)}, bf16[1,256,3584]{1,2,0:T(8,128)(2,1)}, u32[]{:S(2)}) copy-start(bf16[1,256,3584]{1,2,0:T(8,128)(2,1)} %copy.75) | copy-start | bytes 5505028
  350.2 4.5 copy-start.6
  359.3 5.7 copy-start.4
  359.3 98.0 %all-to-all-start.3 = ((bf16[4,1152,896]{2,1,0:T(8,128)(2,1)}), bf16[4,1152,896]{2,1,0:T(8,128)(2,1)}, u32[]{:S(2)}, u32[]{:S(2)}) async-start(bf16[4,1152,896]{2,1,0:T(8,128)(2,1)} %fusion.2), calls=%async_computation.3 | async-start | bytes 16515072 | tf_op jit(solution)/shard_map/all_to_all | solution.py:83
  457.3 23.3 %all-to-all-start.5 = ((bf16[64,1,18]{2,1,0:T(2,128)(2,1)}), bf16[64,1,18]{2,1,0:T(2,128)(2,1)S(1)}, u32[]{:S(2)}, u32[]{:S(2)}) async-start(bf16[64,1,18]{2,1,0:T(2,128)(2,1)} %all_to_all.33), calls=%async_computation.5 | async-start | bytes 65536 | tf_op jit(solution)/shard_map/all_to_all | solution.py:94
  480.5 12.9 %copy-start.7 = (f32[1152,256]{1,0:T(8,128)S(1)}, f32[1152,256]{1,0:T(8,128)}, u32[]{:S(2)}) copy-start(f32[1152,256]{1,0:T(8,128)} %copy-done.6) | copy-start | bytes 3538948
  480.5 80.5 %all-to-all-start.4 = ((bf16[64,18,896]{2,1,0:T(8,128)(2,1)}), bf16[64,18,896]{2,1,0:T(8,128)(2,1)}, u32[]{:S(2)}, u32[]{:S(2)}) async-start(bf16[64,18,896]{2,1,0:T(8,128)(2,1)} %reshape.151), calls=%async_computation.4 | async-start | bytes 5505024 | tf_op jit(solution)/shard_map/all_to_all | solution.py:90
  565.2 12.6 %copy-start.1 = (bf16[1,3584,256]{2,1,0:T(8,128)(2,1)S(1)}, bf16[1,3584,256]{2,1,0:T(8,128)(2,1)}, u32[]{:S(2)}) copy-start(bf16[1,3584,256]{2,1,0:T(8,128)(2,1)} %param.10) | copy-start | bytes 5505028
Sparse Core Ops, SparseCore 0:
  120.6 139.6 all-gather.6
  262.1 83.1 all-gather.4

commit v2 on v1

v2 whole, which is shorter than its diff:
```python
import jax
import jax.numpy as jnp
from jax import lax
from jax.sharding import Mesh
from jax.sharding import PartitionSpec as P

DP = ("zlo", "core")


def slot_tables(expert_ids, capacity, experts):
    count, top = expert_ids.shape
    pairs = count * top
    flat = expert_ids.reshape(pairs)
    onehot = flat[:, None] == jnp.arange(experts, dtype=jnp.int32)[None, :]
    earlier = (
        jnp.arange(pairs, dtype=jnp.int32)[None, :] < jnp.arange(pairs, dtype=jnp.int32)[:, None]
    ).astype(jnp.bfloat16)
    counts = jnp.dot(earlier, onehot.astype(jnp.bfloat16), preferred_element_type=jnp.float32)
    slot = jnp.sum(jnp.where(onehot, counts, 0.0), axis=1).astype(jnp.int32)
    target = flat * capacity + slot
    placing = (target[:, None] == jnp.arange(experts * capacity, dtype=jnp.int32)[None, :]).astype(
        jnp.float32
    )
    picker = jnp.sum(placing.reshape(count, top, experts * capacity), axis=1)
    return (target, placing, picker)


def expert_terms(all_x, all_u, rows_p, block_in, block_out):
    n_c, n_z, rows, part = all_x.shape
    ff = block_in.shape[1]
    w_in_q = block_in.reshape(n_z, n_c, part, ff)
    w_out_q = block_out.reshape(ff, n_z, n_c, part)
    hidden = jnp.einsum("czrk,zckf->rf", all_x, w_in_q, preferred_element_type=jnp.float32)
    act = jax.nn.silu(hidden).astype(jnp.bfloat16)
    output = jnp.einsum("rf,fzck->czrk", act, w_out_q, preferred_element_type=jnp.float32)
    score = jnp.sum(output * all_u.astype(jnp.float32), axis=(0, 1, 3))
    scaled = (
        rows_p.astype(jnp.float32)[None, None, :, None] * all_u.astype(jnp.float32)
    ).astype(jnp.bfloat16)
    back = jnp.einsum("czrk,fzck->rf", scaled, w_out_q, preferred_element_type=jnp.float32)
    sigma = jax.nn.sigmoid(hidden)
    inner = (sigma * (1.0 + hidden * (1.0 - sigma)) * back).astype(jnp.bfloat16)
    grad_out = jnp.einsum("rf,czrk->fzck", act, scaled, preferred_element_type=jnp.float32)
    grad_in = jnp.einsum("czrk,rf->zckf", all_x, inner, preferred_element_type=jnp.float32)
    row_grad = jnp.einsum("rf,zckf->zcrk", inner, w_in_q, preferred_element_type=jnp.float32)
    return (
        row_grad,
        score,
        grad_in.reshape(n_z * n_c * part, ff),
        grad_out.reshape(ff, n_z * n_c * part),
    )


def per_device(tokens, cotangent, probs, expert_ids, w_in, w_out):
    count, top = expert_ids.shape
    width = tokens.shape[1]
    n_z = lax.axis_size("zlo")
    n_c = lax.axis_size("core")
    part = width // (n_z * n_c)
    d = lax.axis_index("zlo") * n_c + lax.axis_index("core")
    experts = lax.axis_size("expert") * w_in.shape[0]
    capacity = min(count, max(2, (9 * top * count + 8 * experts - 1) // (8 * experts)))
    block_in = w_in[0]
    block_out = w_out[0]
    target, placing, picker = slot_tables(expert_ids, capacity, experts)
    pick = picker.astype(jnp.bfloat16)
    x_part = lax.dynamic_slice_in_dim(tokens, d * part, part, axis=1)
    u_part = lax.dynamic_slice_in_dim(cotangent, d * part, part, axis=1)
    xu = jnp.concatenate([x_part, u_part], axis=1)
    slot_xu = lax.dot_general(
        pick, xu, (((0,), (0,)), ((), ())), preferred_element_type=jnp.float32
    ).astype(jnp.bfloat16)
    slot_p = jnp.dot(
        probs.reshape(-1).astype(jnp.float32), placing, precision=lax.Precision.HIGHEST
    ).astype(jnp.bfloat16)
    pad = jnp.zeros((experts * capacity, 127), jnp.bfloat16)
    packed = jnp.concatenate([slot_xu, slot_p[:, None], pad], axis=1)
    packed = packed.reshape(experts, capacity, packed.shape[1])
    recv = lax.all_to_all(packed, "expert", split_axis=0, concat_axis=0, tiled=True)
    rows = experts * capacity
    recv = recv.reshape(rows, recv.shape[2])
    recv_xu = recv[:, : 2 * part]
    recv_p = recv[:, 2 * part]
    pair_xu = lax.all_gather(recv_xu, "zlo", axis=0, tiled=False)
    all_xu = lax.all_gather(pair_xu, "core", axis=0, tiled=False)
    all_x = all_xu[..., :part]
    all_u = all_xu[..., part:]
    row_grad, score, grad_in, grad_out = expert_terms(all_x, all_u, recv_p, block_in, block_out)
    on_chip = lax.all_to_all(
        row_grad.astype(jnp.bfloat16), "core", split_axis=1, concat_axis=1, tiled=True
    )
    chip_sum = jnp.sum(on_chip.astype(jnp.float32), axis=1).astype(jnp.bfloat16)
    off_chip = lax.all_to_all(chip_sum, "zlo", split_axis=0, concat_axis=0, tiled=True)
    row_sum = jnp.sum(off_chip.astype(jnp.float32), axis=0).astype(jnp.bfloat16)
    score_all = lax.all_gather(score.astype(jnp.bfloat16), DP, axis=0, tiled=False)
    score_sum = jnp.sum(score_all.astype(jnp.float32), axis=0)
    back_x, back_s = (
        lax.all_to_all(
            row_sum.reshape(experts, capacity, part), "expert", split_axis=0, concat_axis=0,
            tiled=True,
        ),
        lax.all_to_all(
            score_sum.astype(jnp.bfloat16).reshape(experts, capacity), "expert", split_axis=0,
            concat_axis=0, tiled=True,
        ),
    )
    token_part = jnp.dot(
        pick, back_x.reshape(experts * capacity, part), preferred_element_type=jnp.float32
    )
    grad_tokens = lax.all_gather(token_part.astype(jnp.bfloat16), DP, axis=1, tiled=True)
    gate_grad = (
        jnp.take(back_s.reshape(-1).astype(jnp.float32), target).reshape(count, top)
    ).astype(jnp.bfloat16)
    grad_w_in = grad_in.astype(jnp.bfloat16)[None]
    grad_w_out = grad_out.astype(jnp.bfloat16)[None]
    return (grad_tokens, gate_grad, grad_w_in, grad_w_out)


def solution(mesh):
    n_dp, n_ex = mesh.devices.shape
    split = Mesh(mesh.devices.reshape(2, n_dp // 2, n_ex), ("zlo", "core", "expert"))
    in_specs = (
        P("expert", None),
        P("expert", None),
        P("expert", None),
        P("expert", None),
        P("expert", None, DP),
        P("expert", DP, None),
    )
    out_specs = (
        P("expert", None),
        P("expert", None),
        P("expert", None, DP),
        P("expert", DP, None),
    )
    return jax.shard_map(
        per_device, mesh=split, in_specs=in_specs, out_specs=out_specs, check_vma=False
    )
```

time: 586 us -> 567 us (0.968)
  blocking collectives: 281 us -> 219 us
  waiting for transfers between devices: 124 us -> 174 us
  local copies, waits for them, and re-layouts: 60.3 us -> 76.1 us
  other arithmetic: 26.5 us -> 15.4 us
  starting transfers between devices: 35.8 us -> 29.2 us
    all_gather x2, waiting for transfers between devices: 77.1 us -> 130 us  [the longest x1 103 us: per_device(): pair_xu = lax.all_gather(recv_xu, 'zlo', axis=0, tiled=False)]
    all_gather x2, blocking collectives: 94.4 us -> 52.3 us  [the longest x1 42.9 us: per_device(): lax.all_gather(score.astype(jnp.bfloat16), DP, axis=0, tiled=False)]
    all_to_all x2, blocking collectives: 187 us -> 167 us  [the longest x1 149 us: per_device(): lax.all_to_all(packed, 'expert', split_axis=0, concat_axis=0, tiled=True)]
    another operation x3 -> x0, other arithmetic: 18.2 us -> none
    concatenate x0 -> x3, local copies, waits for them, and re-layouts: none -> 16.8 us  [per_device(): packed = jnp.concatenate([slot_xu, slot_p[:, None], pad], axis=1)]
    all_gather x1 -> x0, local copies, waits for them, and re-layouts: 11.5 us -> none  [per_device(): lax.all_gather(recv_u.reshape(rows, part), 'dp', axis=0, tiled=False)]
    convert_element_type x1 -> x3, local copies, waits for them, and re-layouts: 0.13 us -> 9.65 us  [the longest x1 7.17 us: per_device(): row_grad.astype(jnp.bfloat16)]
    all_to_all x2 -> x1, waiting for transfers between devices: 7.26 us -> 0.01 us  [per_device(): lax.all_to_all(chip_sum, 'zlo', split_axis=0, concat_axis=0, tiled=True)]
  transfers between devices with their start and end apart: 6 -> 5, of which waited for: 5 -> 4; matrix products, arithmetic and copies ran while one was open for 12% -> 9% of each run, Pallas kernels for 0% -> 0%
where the time goes in v2:
time: 567 us; the launch traced here: 565 us
  blocking collectives  219 us (39%)
  waiting for transfers between devices  174 us (31%)
  local copies, waits for them, and re-layouts  76.1 us (13%)
  matrix products  37.2 us (7%)
  starting transfers between devices  29.2 us (5%)
  other arithmetic  15.4 us (3%)
  between operations  14.3 us (3%)
    all_to_all x1, blocking collectives, per_device(): lax.all_to_all(packed, 'expert', split_axis=0, concat_axis=0, tiled=True)  149 us
    all_gather x1, waiting for transfers between devices, per_device(): pair_xu = lax.all_gather(recv_xu, 'zlo', axis=0, tiled=False)  103 us
    all_gather x1, blocking collectives, per_device(): lax.all_gather(score.astype(jnp.bfloat16), DP, axis=0, tiled=False)  42.9 us
    all_to_all x1, waiting for transfers between devices, per_device(): lax.all_to_all(row_sum.reshape(experts, capacity, part), 'expert', split_...  42.6 us
    all_gather x1, waiting for transfers between devices, per_device(): all_xu = lax.all_gather(pair_xu, 'core', axis=0, tiled=False)  26.6 us
    all_to_all x1, blocking collectives, per_device(): lax.all_to_all(row_grad.astype(jnp.bfloat16), 'core', split_axis=1, conca...  18.1 us
    concatenate x3, local copies, waits for them, and re-layouts, per_device(): packed = jnp.concatenate([slot_xu, slot_p[:, None], pad], axis=1)  16.8 us
    all_to_all x1, starting transfers between devices, per_device(): lax.all_to_all(score_sum.astype(jnp.bfloat16).reshape(experts, capacity),...  12.6 us
  transfers between devices with their start and end apart: 5, of which 4 were waited for; matrix products, arithmetic and copies ran while one was open for 9% of the time, Pallas kernels for 0%

profile of v2, /device:TPU:1, one launch (start us, length us, event | category | flops | bytes accessed | tf_op | source)
XLA Modules:
  0.0 565.3 jit_solution(17061378609028837846)
XLA Ops:
  13.7 3.2 convolution_convert_fusion.1
  16.9 7.2 %concatenate.12 = bf16[64,18,1792]{2,1,0:T(8,128)(2,1)} reshape(bf16[1152,1792]{1,0:T(8,128)(2,1)} %convolution_convert_fusion.1) | data formatting | bytes 8257536 | tf_op jit(solution)/shard_map/concatenate | solution.py:77
  24.1 9.3 %concatenate.14 = bf16[64,18,1920]{2,1,0:T(8,128)(2,1)} concatenate(bf16[64,18,1792]{2,1,0:T(8,128)(2,1)} %concatenate.12, bf16[64,18,1]{2,1,0:T(8,128)(2,1)S(1)} %concatenate.15, bf16[64,18,127]{2,1,0:T(8,128)(2,1)S(1)} %broadcast_in_dim.11), dimensions={2} | concatenate | bytes 8847360 | tf_op jit(solution)/shard_map/concatenate | solution.py:77
  33.4 148.7 %all_to_all.30 = bf16[64,18,1920]{2,1,0:T(8,128)(2,1)} all-to-all(bf16[64,18,1920]{2,1,0:T(8,128)(2,1)} %concatenate.14), channel_id=1, replica_groups=mesh['zlo'=2,'core'=2,'expert'=64] {'expert'}, dimensions={0} | all-to-all | bytes 8847360 | tf_op jit(solution)/shard_map/all_to_all | solution.py:79
  182.1 7.5 %reshape.133 = bf16[1152,1920]{1,0:T(8,128)(2,1)} reshape(bf16[64,18,1920]{2,1,0:T(8,128)(2,1)} %all_to_all.30) | data formatting | bytes 8847360 | tf_op jit(solution)/shard_map/reshape | solution.py:81
  189.6 4.4 slice.18
  194.2 103.3 %all-gather.7.cloned.1.call-done = bf16[2304,1792]{1,0:T(8,128)(2,1)} async-done(((bf16[1152,1792]{1,0:T(8,128)(2,1)}), bf16[2304,1792]{1,0:T(8,128)(2,1)}) %all-gather.7.cloned.1.call-update) | async-done | bytes 8257552 | tf_op jit(solution)/shard_map/all_gather | solution.py:84
  297.5 4.9 reshape_squeeze.7
  302.4 5.5 copy.54
  309.0 26.6 %all-gather.9.cloned.1.call-done = bf16[4,1152,1792]{2,1,0:T(8,128)(2,1)} async-done(((bf16[2,1152,1792]{2,1,0:T(8,128)(2,1)}), bf16[4,1152,1792]{2,1,0:T(8,128)(2,1)}) %all-gather.9.cloned.1.call-update) | async-done | bytes 16515088 | tf_op jit(solution)/shard_map/all_gather | solution.py:85
  335.6 4.9 fusion.9
  340.5 3.8 copy-done.4
  344.3 2.9 fusion.14
  347.3 4.5 fusion.2
  351.8 7.2 %copy.53 = bf16[2,2,1152,896]{3,2,0,1:T(8,128)(2,1)} copy(bf16[2,2,1152,896]{3,2,1,0:T(8,128)(2,1)} %fusion.2) | data formatting | bytes 16515072 | tf_op jit(solution)/shard_map/convert_element_type | solution.py:90
  359.0 18.1 %all_to_all.31 = bf16[2,2,1152,896]{3,2,0,1:T(8,128)(2,1)} all-to-all(bf16[2,2,1152,896]{3,2,0,1:T(8,128)(2,1)} %copy.53), channel_id=1, replica_groups=mesh['zlo'=2,'core'=2,'expert'=64] {'core'}, dimensions={1} | all-to-all | bytes 16515072 | tf_op jit(solution)/shard_map/all_to_all | solution.py:89
  377.1 7.8 %reduce_sum.65 = bf16[2,1152,896]{2,1,0:T(8,128)(2,1)} reduce(bf16[2,2,1152,896]{3,2,0,1:T(8,128)(2,1)} %all_to_all.31, bf16[]{:T(256)} %constant.42.clone.1), dimensions={1}, to_apply=%region_2.3 | reduce | flops 2064384 | bytes 12386306 | tf_op jit(solution)/shard_map/reduce_sum | solution.py:92
  384.8 5.7 %all-to-all-start.2 = ((bf16[2,1152,896]{2,1,0:T(8,128)(2,1)}), bf16[2,1152,896]{2,1,0:T(8,128)(2,1)}, u32[]{:S(2)}, u32[]{:S(2)}) async-start(bf16[2,1152,896]{2,1,0:T(8,128)(2,1)} %reduce_sum.65), calls=%async_computation.2 | async-start | bytes 8257536 | tf_op jit(solution)/shard_map/all_to_all | solution.py:93
  390.6 5.5 fusion.1
  396.1 42.9 %all-gather.3 = bf16[4,1,1152]{2,1,0:T(2,128)(2,1)S(1)} all-gather(bf16[1,1,1152]{2,1,0:T(2,128)(2,1)S(1)} %reshape.149), channel_id=4, replica_groups=mesh['zlo'=2,'core'=2,'expert'=64] {'zlo','core'}, dimensions={0}, use_global_device_ids=true | all-gather | bytes 11520 | tf_op jit(solution)/shard_map/all_gather | solution.py:95
  439.8 12.6 %all-to-all-start.4 = ((bf16[64,1,18]{2,1,0:T(2,128)(2,1)}), bf16[64,1,18]{2,1,0:T(2,128)(2,1)S(1)}, u32[]{:S(2)}, u32[]{:S(2)}) async-start(bf16[64,1,18]{2,1,0:T(2,128)(2,1)} %all_to_all.24), calls=%async_computation.4 | async-start | bytes 65536 | tf_op jit(solution)/shard_map/all_to_all | solution.py:102
  452.3 4.9 reduce_sum.66
  457.2 4.1 reshape.134
  462.9 10.7 %all-to-all-start.3 = ((bf16[64,18,896]{2,1,0:T(8,128)(2,1)}), bf16[64,18,896]{2,1,0:T(8,128)(2,1)}, u32[]{:S(2)}, u32[]{:S(2)}) async-start(bf16[64,18,896]{2,1,0:T(8,128)(2,1)} %reshape.134), calls=%async_computation.3 | async-start | bytes 5505024 | tf_op jit(solution)/shard_map/all_to_all | solution.py:98
  473.7 5.9 %convert_bitcast_fusion.1 = bf16[2,2,896,256]{2,3,0,1:T(8,128)(2,1)S(1)} fusion(bf16[1152,256,1,1]{1,0,3,2:T(8,128)(2,1)S(1)} %fusion.14, bf16[2,2,1152,1792]{3,2,1,0:T(8,128)(2,1)} %bitcast.59), kind=kOutput, calls=%fused_computation.27 | convolution fusion | flops 2114846720 | bytes 10682368 | tf_op jit(solution)/shard_map/czrk,rf->zckf/dot_general | solution.py:44
  479.6 2.4 copy.58
  482.0 6.6 %convert_bitcast_fusion = bf16[256,2,2,896]{0,3,1,2:T(8,128)(2,1)S(1)} fusion(f32[1152]{0:T(1024)S(1)} %convert_reduce_fusion.1, bf16[2,2,1152,1792]{3,2,1,0:T(8,128)(2,1)} %bitcast.60, f32[1152,256]{1,0:T(8,128)} %copy-done.5), kind=kOutput, calls=%fused_computation.26 | convolution fusion | flops 2128707584 | bytes 11276800 | tf_op jit(solution)/shard_map/rf,czrk->fzck/dot_general | solution.py:43
  488.7 2.6 copy.62
  491.5 6.8 %gather_fusion = bf16[1024]{0:T(1024)(128)(2,1)S(1)} fusion(bf16[1152]{0:T(1024)(128)(2,1)S(1)} %reshape.137, s32[1024]{0:T(1024)S(1)} %broadcast_clamp_fusion), kind=kCustom, calls=%fused_computation | custom fusion | bytes 8192 | tf_op jit(solution)/shard_map/jit(_take)/gather | solution.py:112
  499.1 42.6 %all-to-all-done.3 = bf16[64,18,896]{2,1,0:T(8,128)(2,1)} async-done(((bf16[64,18,896]{2,1,0:T(8,128)(2,1)}), bf16[64,18,896]{2,1,0:T(8,128)(2,1)}, u32[]{:S(2)}, u32[]{:S(2)}) %all-to-all-start.3) | async-done | bytes 2064416 | tf_op jit(solution)/shard_map/all_to_all | solution.py:98
  541.8 4.2 reshape.135
  548.1 9.4 %all_gather.23 = bf16[128,3584]{1,0:T(8,128)(2,1)S(1)} all-gather(bf16[128,896]{1,0:T(8,128)(2,1)S(1)} %convolution_convert_fusion.2), channel_id=1, replica_groups=mesh['zlo'=2,'core'=2,'expert'=64] {'zlo','core'}, dimensions={1}, use_global_device_ids=true | all-gather | bytes 1146880 | tf_op jit(solution)/shard_map/all_gather | solution.py:110
  (46 shorter events, 14.6 us)
Async XLA Ops:
  7.2 328.5 %copy-start = (bf16[1,3584,256]{2,1,0:T(8,128)(2,1)S(1)}, bf16[1,3584,256]{2,1,0:T(8,128)(2,1)}, u32[]{:S(2)}) copy-start(bf16[1,3584,256]{2,1,0:T(8,128)(2,1)} %param.10) | copy-start | bytes 5505028
  7.2 290.3 %all-gather.7.cloned.1.call-start = ((), (), s32[]{:S(2)}) async-start(), calls=%async_computation.5 | async-start | bytes 12386304 | tf_op jit(solution)/shard_map/all_gather | solution.py:84
  193.9 141.7 %all-gather.9.cloned.1.call-start = ((), (), s32[]{:S(2)}) async-start(), calls=%async_computation.6 | async-start | bytes 24772608 | tf_op jit(solution)/shard_map/all_gather | solution.py:85
  335.6 4.9 copy-start.2
  335.6 8.7 %copy-start.4 = (bf16[4,1152,1792]{2,1,0:T(8,128)(2,1)S(1)}, bf16[4,1152,1792]{2,1,0:T(8,128)(2,1)}, u32[]{:S(2)}) copy-start(bf16[4,1152,1792]{2,1,0:T(8,128)(2,1)} %all-gather.9.cloned.1.call-done) | copy-start | bytes 49545220
  344.3 2.9 copy-start.5
  384.8 5.7 %copy-start.3 = (bf16[256,2,2,896]{0,3,1,2:T(8,128)(2,1)S(1)}, bf16[256,2,2,896]{0,3,1,2:T(8,128)(2,1)}, u32[]{:S(2)}) copy-start(bf16[256,2,2,896]{0,3,1,2:T(8,128)(2,1)} %copy.54) | copy-start | bytes 5505028
  384.8 54.9 %all-to-all-start.2 = ((bf16[2,1152,896]{2,1,0:T(8,128)(2,1)}), bf16[2,1152,896]{2,1,0:T(8,128)(2,1)}, u32[]{:S(2)}, u32[]{:S(2)}) async-start(bf16[2,1152,896]{2,1,0:T(8,128)(2,1)} %reduce_sum.65), calls=%async_computation.2 | async-start | bytes 8257536 | tf_op jit(solution)/shard_map/all_to_all | solution.py:93
  439.8 23.1 %all-to-all-start.4 = ((bf16[64,1,18]{2,1,0:T(2,128)(2,1)}), bf16[64,1,18]{2,1,0:T(2,128)(2,1)S(1)}, u32[]{:S(2)}, u32[]{:S(2)}) async-start(bf16[64,1,18]{2,1,0:T(2,128)(2,1)} %all_to_all.24), calls=%async_computation.4 | async-start | bytes 65536 | tf_op jit(solution)/shard_map/all_to_all | solution.py:102
  462.9 78.9 %all-to-all-start.3 = ((bf16[64,18,896]{2,1,0:T(8,128)(2,1)}), bf16[64,18,896]{2,1,0:T(8,128)(2,1)}, u32[]{:S(2)}, u32[]{:S(2)}) async-start(bf16[64,18,896]{2,1,0:T(8,128)(2,1)} %reshape.134), calls=%async_computation.3 | async-start | bytes 5505024 | tf_op jit(solution)/shard_map/all_to_all | solution.py:98
  545.9 12.6 %copy-start.1 = (bf16[1,3584,256]{2,1,0:T(8,128)(2,1)S(1)}, bf16[1,3584,256]{2,1,0:T(8,128)(2,1)}, u32[]{:S(2)}) copy-start(bf16[1,3584,256]{2,1,0:T(8,128)(2,1)} %param.10) | copy-start | bytes 5505028
Sparse Core Ops, SparseCore 0:
  194.1 103.3 all-gather.6
  299.3 36.2 all-gather.8

commit v3 on v2

--- a/solution.py
+++ b/solution.py
@@ -75,10 +75,11 @@
     ).astype(jnp.bfloat16)
     pad = jnp.zeros((experts * capacity, 127), jnp.bfloat16)
     packed = jnp.concatenate([slot_xu, slot_p[:, None], pad], axis=1)
-    packed = packed.reshape(experts, capacity, packed.shape[1])
+    lanes = packed.shape[1]
+    packed = packed.reshape(experts, capacity * lanes // 128, 128)
     recv = lax.all_to_all(packed, "expert", split_axis=0, concat_axis=0, tiled=True)
     rows = experts * capacity
-    recv = recv.reshape(rows, recv.shape[2])
+    recv = recv.reshape(rows, lanes)
     recv_xu = recv[:, : 2 * part]
     recv_p = recv[:, 2 * part]
     pair_xu = lax.all_gather(recv_xu, "zlo", axis=0, tiled=False)
@@ -96,8 +97,8 @@
     score_sum = jnp.sum(score_all.astype(jnp.float32), axis=0)
     back_x, back_s = (
         lax.all_to_all(
-            row_sum.reshape(experts, capacity, part), "expert", split_axis=0, concat_axis=0,
-            tiled=True,
+            row_sum.reshape(experts, capacity * part // 128, 128), "expert", split_axis=0,
+            concat_axis=0, tiled=True,
         ),
         lax.all_to_all(
             score_sum.astype(jnp.bfloat16).reshape(experts, capacity), "expert", split_axis=0,

time: 567 us -> 523 us (0.922)
  blocking collectives: 219 us -> 188 us
  waiting for transfers between devices: 174 us -> 159 us
    all_to_all x1, blocking collectives: 149 us -> 118 us  [per_device(): lax.all_to_all(packed, 'expert', split_axis=0, concat_axis=0, tiled=True)]
    all_to_all x1, waiting for transfers between devices: 42.6 us -> 27.3 us  [per_device(): lax.all_to_all(row_sum.reshape(experts, capacity * part // 128, 128), 'ex...]
    reshape x2 -> x3, local copies, waits for them, and re-layouts: 11.6 us -> 22.6 us  [the longest x1 9.13 us: per_device(): packed = packed.reshape(experts, capacity * lanes // 128, 128)]
    concatenate x3 -> x1, local copies, waits for them, and re-layouts: 16.8 us -> 7.37 us  [per_device(): packed = jnp.concatenate([slot_xu, slot_p[:, None], pad], axis=1)]
  transfers between devices with their start and end apart: 5 -> 5, of which waited for: 4 -> 4; matrix products, arithmetic and copies ran while one was open for 9% -> 10% of each run, Pallas kernels for 0% -> 0%
where the time goes in v3:
time: 523 us; the launch traced here: 522 us
  blocking collectives  188 us (36%)
  waiting for transfers between devices  159 us (30%)
  local copies, waits for them, and re-layouts  78.4 us (15%)
  matrix products  37.3 us (7%)
  starting transfers between devices  29.7 us (6%)
  other arithmetic  15.4 us (3%)
  between operations  14.3 us (3%)
    all_to_all x1, blocking collectives, per_device(): lax.all_to_all(packed, 'expert', split_axis=0, concat_axis=0, tiled=True)  118 us
    all_gather x1, waiting for transfers between devices, per_device(): pair_xu = lax.all_gather(recv_xu, 'zlo', axis=0, tiled=False)  104 us
    all_gather x1, blocking collectives, per_device(): lax.all_gather(score.astype(jnp.bfloat16), DP, axis=0, tiled=False)  42.9 us
    all_to_all x1, waiting for transfers between devices, per_device(): lax.all_to_all(row_sum.reshape(experts, capacity * part // 128, 128), 'ex...  27.3 us
    all_gather x1, waiting for transfers between devices, per_device(): all_xu = lax.all_gather(pair_xu, 'core', axis=0, tiled=False)  26.6 us
    all_to_all x1, blocking collectives, per_device(): lax.all_to_all(row_grad.astype(jnp.bfloat16), 'core', split_axis=1, conca...  18.1 us
    all_to_all x1, starting transfers between devices, per_device(): lax.all_to_all(score_sum.astype(jnp.bfloat16).reshape(experts, capacity),...  12.6 us
    all_to_all x1, starting transfers between devices, per_device(): lax.all_to_all(row_sum.reshape(experts, capacity * part // 128, 128), 'ex...  11.2 us
  transfers between devices with their start and end apart: 5, of which 4 were waited for; matrix products, arithmetic and copies ran while one was open for 10% of the time, Pallas kernels for 0%

profile of v3, /device:TPU:1, one launch (start us, length us, event | category | flops | bytes accessed | tf_op | source)
XLA Modules:
  0.0 521.8 jit_solution(12752050494655985936)
XLA Ops:
  13.6 3.2 convolution_convert_fusion.1
  16.8 7.4 %concatenate.7 = bf16[1152,1920]{1,0:T(8,128)(2,1)} concatenate(bf16[1152,1792]{1,0:T(8,128)(2,1)} %convolution_convert_fusion.1, bf16[1152,1]{1,0:T(8,128)(2,1)S(1)} %broadcast_in_dim.28, bf16[1152,127]{1,0:T(8,128)(2,1)S(1)} %broadcast_in_dim.26), dimensions={1} | concatenate | bytes 8847360 | tf_op jit(solution)/shard_map/concatenate | solution.py:77
  24.2 9.1 %reshape.131 = bf16[64,270,128]{2,1,0:T(8,128)(2,1)} reshape(bf16[1152,1920]{1,0:T(8,128)(2,1)} %concatenate.7) | data formatting | bytes 8847360 | tf_op jit(solution)/shard_map/reshape | solution.py:79
  33.3 117.5 %all_to_all.30 = bf16[64,270,128]{2,1,0:T(8,128)(2,1)} all-to-all(bf16[64,270,128]{2,1,0:T(8,128)(2,1)} %reshape.131), channel_id=1, replica_groups=mesh['zlo'=2,'core'=2,'expert'=64] {'expert'}, dimensions={0} | all-to-all | bytes 8847360 | tf_op jit(solution)/shard_map/all_to_all | solution.py:80
  150.8 8.9 %reshape.132 = bf16[1152,1920]{1,0:T(8,128)(2,1)} reshape(bf16[64,270,128]{2,1,0:T(8,128)(2,1)} %all_to_all.30) | data formatting | bytes 8847360 | tf_op jit(solution)/shard_map/reshape | solution.py:82
  159.7 4.4 slice.18
  164.3 103.8 %all-gather.7.cloned.1.call-done = bf16[2304,1792]{1,0:T(8,128)(2,1)} async-done(((bf16[1152,1792]{1,0:T(8,128)(2,1)}), bf16[2304,1792]{1,0:T(8,128)(2,1)}) %all-gather.7.cloned.1.call-update) | async-done | bytes 8257552 | tf_op jit(solution)/shard_map/all_gather | solution.py:85
  268.2 4.9 reshape_squeeze.7
  273.1 5.5 %copy.54 = bf16[256,2,2,896]{0,3,1,2:T(8,128)(2,1)} copy(bf16[256,2,2,896]{3,2,1,0:T(2,128)(2,1)} %reshape_squeeze.7) | data formatting | bytes 3670016 | tf_op jit(solution)/shard_map/reshape;squeeze | solution.py:32
  279.7 26.6 %all-gather.9.cloned.1.call-done = bf16[4,1152,1792]{2,1,0:T(8,128)(2,1)} async-done(((bf16[2,1152,1792]{2,1,0:T(8,128)(2,1)}), bf16[4,1152,1792]{2,1,0:T(8,128)(2,1)}) %all-gather.9.cloned.1.call-update) | async-done | bytes 16515088 | tf_op jit(solution)/shard_map/all_gather | solution.py:86
  306.3 4.9 fusion.9
  311.2 3.8 copy-done.4
  315.0 2.9 fusion.14
  318.0 4.5 fusion.2
  322.5 7.2 %copy.53 = bf16[2,2,1152,896]{3,2,0,1:T(8,128)(2,1)} copy(bf16[2,2,1152,896]{3,2,1,0:T(8,128)(2,1)} %fusion.2) | data formatting | bytes 16515072 | tf_op jit(solution)/shard_map/convert_element_type | solution.py:91
  329.7 18.1 %all_to_all.31 = bf16[2,2,1152,896]{3,2,0,1:T(8,128)(2,1)} all-to-all(bf16[2,2,1152,896]{3,2,0,1:T(8,128)(2,1)} %copy.53), channel_id=1, replica_groups=mesh['zlo'=2,'core'=2,'expert'=64] {'core'}, dimensions={1} | all-to-all | bytes 16515072 | tf_op jit(solution)/shard_map/all_to_all | solution.py:90
  347.8 7.8 %reduce_sum.65 = bf16[2,1152,896]{2,1,0:T(8,128)(2,1)} reduce(bf16[2,2,1152,896]{3,2,0,1:T(8,128)(2,1)} %all_to_all.31, bf16[]{:T(256)} %constant.42.clone.1), dimensions={1}, to_apply=%region_2.3 | reduce | flops 2064384 | bytes 12386306 | tf_op jit(solution)/shard_map/reduce_sum | solution.py:93
  355.5 5.7 %all-to-all-start.2 = ((bf16[2,1152,896]{2,1,0:T(8,128)(2,1)}), bf16[2,1152,896]{2,1,0:T(8,128)(2,1)}, u32[]{:S(2)}, u32[]{:S(2)}) async-start(bf16[2,1152,896]{2,1,0:T(8,128)(2,1)} %reduce_sum.65), calls=%async_computation.2 | async-start | bytes 8257536 | tf_op jit(solution)/shard_map/all_to_all | solution.py:94
  361.3 5.5 %fusion.1 = bf16[1152]{0:T(1024)(128)(2,1)S(1)} fusion(bf16[256,2,2,896]{0,3,1,2:T(8,128)(2,1)S(1)} %copy-done.3, bf16[2,2,1152,1792]{3,2,1,0:T(8,128)(2,1)} %bitcast.58, f32[1152,256]{1,0:T(8,128)} %copy-done.5), kind=kOutput, calls=%fused_computation.4 | convolution fusion | flops 2127788928 | bytes 11274496 | tf_op jit(solution)/shard_map/rf,fzck->czrk/dot_general | solution.py:35
  366.8 42.9 %all-gather.3 = bf16[4,1,1152]{2,1,0:T(2,128)(2,1)S(1)} all-gather(bf16[1,1,1152]{2,1,0:T(2,128)(2,1)S(1)} %reshape.148), channel_id=4, replica_groups=mesh['zlo'=2,'core'=2,'expert'=64] {'zlo','core'}, dimensions={0}, use_global_device_ids=true | all-gather | bytes 11520 | tf_op jit(solution)/shard_map/all_gather | solution.py:96
  410.5 12.6 %all-to-all-start.4 = ((bf16[64,1,18]{2,1,0:T(2,128)(2,1)}), bf16[64,1,18]{2,1,0:T(2,128)(2,1)S(1)}, u32[]{:S(2)}, u32[]{:S(2)}) async-start(bf16[64,1,18]{2,1,0:T(2,128)(2,1)} %all_to_all.24), calls=%async_computation.4 | async-start | bytes 65536 | tf_op jit(solution)/shard_map/all_to_all | solution.py:103
  423.0 4.9 reduce_sum.66
  427.9 4.6 reshape.133
  433.6 11.2 %all-to-all-start.3 = ((bf16[64,126,128]{2,1,0:T(8,128)(2,1)}), bf16[64,126,128]{2,1,0:T(8,128)(2,1)}, u32[]{:S(2)}, u32[]{:S(2)}) async-start(bf16[64,126,128]{2,1,0:T(8,128)(2,1)} %reshape.133), calls=%async_computation.3 | async-start | bytes 4194304 | tf_op jit(solution)/shard_map/all_to_all | solution.py:99
  444.9 5.9 %convert_bitcast_fusion.1 = bf16[2,2,896,256]{2,3,0,1:T(8,128)(2,1)S(1)} fusion(bf16[1152,256,1,1]{1,0,3,2:T(8,128)(2,1)S(1)} %fusion.14, bf16[2,2,1152,1792]{3,2,1,0:T(8,128)(2,1)} %bitcast.59), kind=kOutput, calls=%fused_computation.27 | convolution fusion | flops 2114846720 | bytes 10682368 | tf_op jit(solution)/shard_map/czrk,rf->zckf/dot_general | solution.py:44
  450.8 2.4 copy.58
  453.2 6.6 %convert_bitcast_fusion = bf16[256,2,2,896]{0,3,1,2:T(8,128)(2,1)S(1)} fusion(f32[1152]{0:T(1024)S(1)} %convert_reduce_fusion.1, bf16[2,2,1152,1792]{3,2,1,0:T(8,128)(2,1)} %bitcast.60, f32[1152,256]{1,0:T(8,128)} %copy-done.5), kind=kOutput, calls=%fused_computation.26 | convolution fusion | flops 2128707584 | bytes 11276800 | tf_op jit(solution)/shard_map/rf,czrk->fzck/dot_general | solution.py:43
  459.9 2.6 copy.62
  462.7 6.8 %gather_fusion = bf16[1024]{0:T(1024)(128)(2,1)S(1)} fusion(bf16[1152]{0:T(1024)(128)(2,1)S(1)} %reshape.136, s32[1024]{0:T(1024)S(1)} %broadcast_clamp_fusion), kind=kCustom, calls=%fused_computation | custom fusion | bytes 8192 | tf_op jit(solution)/shard_map/jit(_take)/gather | solution.py:113
  470.3 27.3 %all-to-all-done.3 = bf16[64,126,128]{2,1,0:T(8,128)(2,1)} async-done(((bf16[64,126,128]{2,1,0:T(8,128)(2,1)}), bf16[64,126,128]{2,1,0:T(8,128)(2,1)}, u32[]{:S(2)}, u32[]{:S(2)}) %all-to-all-start.3) | async-done | bytes 2064416 | tf_op jit(solution)/shard_map/all_to_all | solution.py:99
  497.6 4.7 reshape.134
  504.6 9.4 %all_gather.23 = bf16[128,3584]{1,0:T(8,128)(2,1)S(1)} all-gather(bf16[128,896]{1,0:T(8,128)(2,1)S(1)} %convolution_convert_fusion.2), channel_id=1, replica_groups=mesh['zlo'=2,'core'=2,'expert'=64] {'zlo','core'}, dimensions={1}, use_global_device_ids=true | all-gather | bytes 1146880 | tf_op jit(solution)/shard_map/all_gather | solution.py:111
  (46 shorter events, 14.1 us)
Async XLA Ops:
  7.2 299.1 %copy-start = (bf16[1,3584,256]{2,1,0:T(8,128)(2,1)S(1)}, bf16[1,3584,256]{2,1,0:T(8,128)(2,1)}, u32[]{:S(2)}) copy-start(bf16[1,3584,256]{2,1,0:T(8,128)(2,1)} %param.10) | copy-start | bytes 5505028
  7.2 261.0 %all-gather.7.cloned.1.call-start = ((), (), s32[]{:S(2)}) async-start(), calls=%async_computation.5 | async-start | bytes 12386304 | tf_op jit(solution)/shard_map/all_gather | solution.py:85
  164.1 142.2 %all-gather.9.cloned.1.call-start = ((), (), s32[]{:S(2)}) async-start(), calls=%async_computation.6 | async-start | bytes 24772608 | tf_op jit(solution)/shard_map/all_gather | solution.py:86
  306.3 4.9 copy-start.2
  306.3 8.7 %copy-start.4 = (bf16[4,1152,1792]{2,1,0:T(8,128)(2,1)S(1)}, bf16[4,1152,1792]{2,1,0:T(8,128)(2,1)}, u32[]{:S(2)}) copy-start(bf16[4,1152,1792]{2,1,0:T(8,128)(2,1)} %all-gather.9.cloned.1.call-done) | copy-start | bytes 49545220
  315.0 2.9 copy-start.5
  355.5 5.7 %copy-start.3 = (bf16[256,2,2,896]{0,3,1,2:T(8,128)(2,1)S(1)}, bf16[256,2,2,896]{0,3,1,2:T(8,128)(2,1)}, u32[]{:S(2)}) copy-start(bf16[256,2,2,896]{0,3,1,2:T(8,128)(2,1)} %copy.54) | copy-start | bytes 5505028
  355.5 54.9 %all-to-all-start.2 = ((bf16[2,1152,896]{2,1,0:T(8,128)(2,1)}), bf16[2,1152,896]{2,1,0:T(8,128)(2,1)}, u32[]{:S(2)}, u32[]{:S(2)}) async-start(bf16[2,1152,896]{2,1,0:T(8,128)(2,1)} %reduce_sum.65), calls=%async_computation.2 | async-start | bytes 8257536 | tf_op jit(solution)/shard_map/all_to_all | solution.py:94
  410.5 23.1 %all-to-all-start.4 = ((bf16[64,1,18]{2,1,0:T(2,128)(2,1)}), bf16[64,1,18]{2,1,0:T(2,128)(2,1)S(1)}, u32[]{:S(2)}, u32[]{:S(2)}) async-start(bf16[64,1,18]{2,1,0:T(2,128)(2,1)} %all_to_all.24), calls=%async_computation.4 | async-start | bytes 65536 | tf_op jit(solution)/shard_map/all_to_all | solution.py:103
  433.6 64.0 %all-to-all-start.3 = ((bf16[64,126,128]{2,1,0:T(8,128)(2,1)}), bf16[64,126,128]{2,1,0:T(8,128)(2,1)}, u32[]{:S(2)}, u32[]{:S(2)}) async-start(bf16[64,126,128]{2,1,0:T(8,128)(2,1)} %reshape.133), calls=%async_computation.3 | async-start | bytes 4194304 | tf_op jit(solution)/shard_map/all_to_all | solution.py:99
  502.3 12.6 %copy-start.1 = (bf16[1,3584,256]{2,1,0:T(8,128)(2,1)S(1)}, bf16[1,3584,256]{2,1,0:T(8,128)(2,1)}, u32[]{:S(2)}) copy-start(bf16[1,3584,256]{2,1,0:T(8,128)(2,1)} %param.10) | copy-start | bytes 5505028
Sparse Core Ops, SparseCore 0:
  164.2 103.9 all-gather.6
  270.0 36.2 all-gather.8

commit v4 on v3

--- a/solution.py
+++ b/solution.py
@@ -25,29 +25,30 @@
     return (target, placing, picker)
 
 
-def expert_terms(all_x, all_u, rows_p, block_in, block_out):
-    n_c, n_z, rows, part = all_x.shape
+def expert_terms(all_x, all_u, rows_p, block_in, block_out, quarters):
+    halves, rows, half = all_x.shape
     ff = block_in.shape[1]
-    w_in_q = block_in.reshape(n_z, n_c, part, ff)
-    w_out_q = block_out.reshape(ff, n_z, n_c, part)
-    hidden = jnp.einsum("czrk,zckf->rf", all_x, w_in_q, preferred_element_type=jnp.float32)
+    w_in_h = block_in.reshape(halves, half, ff)
+    w_out_h = block_out.reshape(ff, halves, half)
+    hidden = jnp.einsum("hrk,hkf->rf", all_x, w_in_h, preferred_element_type=jnp.float32)
     act = jax.nn.silu(hidden).astype(jnp.bfloat16)
-    output = jnp.einsum("rf,fzck->czrk", act, w_out_q, preferred_element_type=jnp.float32)
-    score = jnp.sum(output * all_u.astype(jnp.float32), axis=(0, 1, 3))
-    scaled = (
-        rows_p.astype(jnp.float32)[None, None, :, None] * all_u.astype(jnp.float32)
-    ).astype(jnp.bfloat16)
-    back = jnp.einsum("czrk,fzck->rf", scaled, w_out_q, preferred_element_type=jnp.float32)
+    output = jnp.einsum("rf,fhk->hrk", act, w_out_h, preferred_element_type=jnp.float32)
+    score = jnp.sum(output * all_u.astype(jnp.float32), axis=(0, 2))
+    scaled = (rows_p.astype(jnp.float32)[None, :, None] * all_u.astype(jnp.float32)).astype(
+        jnp.bfloat16
+    )
+    back = jnp.einsum("hrk,fhk->rf", scaled, w_out_h, preferred_element_type=jnp.float32)
     sigma = jax.nn.sigmoid(hidden)
     inner = (sigma * (1.0 + hidden * (1.0 - sigma)) * back).astype(jnp.bfloat16)
-    grad_out = jnp.einsum("rf,czrk->fzck", act, scaled, preferred_element_type=jnp.float32)
-    grad_in = jnp.einsum("czrk,rf->zckf", all_x, inner, preferred_element_type=jnp.float32)
-    row_grad = jnp.einsum("rf,zckf->zcrk", inner, w_in_q, preferred_element_type=jnp.float32)
+    grad_out = jnp.einsum("rf,hrk->fhk", act, scaled, preferred_element_type=jnp.float32)
+    grad_in = jnp.einsum("hrk,rf->hkf", all_x, inner, preferred_element_type=jnp.float32)
+    w_in_q = block_in.reshape(quarters, halves * half // quarters, ff)
+    row_grad = jnp.einsum("rf,qkf->qrk", inner, w_in_q, preferred_element_type=jnp.float32)
     return (
         row_grad,
         score,
-        grad_in.reshape(n_z * n_c * part, ff),
-        grad_out.reshape(ff, n_z * n_c * part),
+        grad_in.reshape(halves * half, ff),
+        grad_out.reshape(ff, halves * half),
     )
 
 
@@ -64,31 +65,37 @@
     block_out = w_out[0]
     target, placing, picker = slot_tables(expert_ids, capacity, experts)
     pick = picker.astype(jnp.bfloat16)
-    x_part = lax.dynamic_slice_in_dim(tokens, d * part, part, axis=1)
-    u_part = lax.dynamic_slice_in_dim(cotangent, d * part, part, axis=1)
-    xu = jnp.concatenate([x_part, u_part], axis=1)
+    c = lax.axis_index("core")
+    half = width // n_c
+    x_half = lax.dynamic_slice_in_dim(tokens, c * half, half, axis=1)
+    u_half = lax.dynamic_slice_in_dim(cotangent, c * half, half, axis=1)
+    xu = jnp.concatenate([x_half, u_half], axis=1)
     slot_xu = lax.dot_general(
         pick, xu, (((0,), (0,)), ((), ())), preferred_element_type=jnp.float32
     ).astype(jnp.bfloat16)
     slot_p = jnp.dot(
         probs.reshape(-1).astype(jnp.float32), placing, precision=lax.Precision.HIGHEST
     ).astype(jnp.bfloat16)
-    pad = jnp.zeros((experts * capacity, 127), jnp.bfloat16)
-    packed = jnp.concatenate([slot_xu, slot_p[:, None], pad], axis=1)
-    lanes = packed.shape[1]
-    packed = packed.reshape(experts, capacity * lanes // 128, 128)
+    body = capacity * 2 * half // 128
+    packed = jnp.concatenate(
+        [
+            slot_xu.reshape(experts, body, 128),
+            jnp.pad(slot_p.reshape(experts, 1, capacity), ((0, 0), (0, 0), (0, 128 - capacity))),
+        ],
+        axis=1,
+    )
     recv = lax.all_to_all(packed, "expert", split_axis=0, concat_axis=0, tiled=True)
     rows = experts * capacity
-    recv = recv.reshape(rows, lanes)
-    recv_xu = recv[:, : 2 * part]
-    recv_p = recv[:, 2 * part]
-    pair_xu = lax.all_gather(recv_xu, "zlo", axis=0, tiled=False)
-    all_xu = lax.all_gather(pair_xu, "core", axis=0, tiled=False)
-    all_x = all_xu[..., :part]
-    all_u = all_xu[..., part:]
-    row_grad, score, grad_in, grad_out = expert_terms(all_x, all_u, recv_p, block_in, block_out)
+    recv_xu = recv[:, :body, :].reshape(rows, 2 * half)
+    recv_p = recv[:, body, :capacity].reshape(rows)
+    all_xu = lax.all_gather(recv_xu, "core", axis=0, tiled=False)
+    all_x = all_xu[..., :half]
+    all_u = all_xu[..., half:]
+    row_grad, score, grad_in, grad_out = expert_terms(
+        all_x, all_u, recv_p, block_in, block_out, n_z * n_c
+    )
     on_chip = lax.all_to_all(
-        row_grad.astype(jnp.bfloat16), "core", split_axis=1, concat_axis=1, tiled=True
+        row_grad.astype(jnp.bfloat16).reshape(n_z, n_c, rows, part), "core", split_axis=1, concat_axis=1, tiled=True
     )
     chip_sum = jnp.sum(on_chip.astype(jnp.float32), axis=1).astype(jnp.bfloat16)
     off_chip = lax.all_to_all(chip_sum, "zlo", split_axis=0, concat_axis=0, tiled=True)

time: 523 us -> 514 us (0.983)
  waiting for transfers between devices: 159 us -> 52.5 us
  blocking collectives: 188 us -> 272 us
    all_gather x2 -> x1, waiting for transfers between devices: 130 us -> 26.4 us  [per_device(): all_xu = lax.all_gather(recv_xu, 'core', axis=0, tiled=False)]
    all_to_all x1, blocking collectives: 118 us -> 201 us  [per_device(): lax.all_to_all(packed, 'expert', split_axis=0, concat_axis=0, tiled=True)]
    another operation x2, local copies, waits for them, and re-layouts: 10.4 us -> 20.4 us  [the longest x1 15.5 us: per_device(): all_xu = lax.all_gather(recv_xu, 'core', axis=0, tiled=False)]
    convert_element_type x2 -> x1, local copies, waits for them, and re-layouts: 9.57 us -> 0.13 us  [expert_terms(): rows_p.astype(jnp.float32)[None, :, None] * all_u.astype(jnp.float32)]
    concatenate x1 -> x0, local copies, waits for them, and re-layouts: 7.37 us -> none  [per_device(): packed = jnp.concatenate([slot_xu, slot_p[:, None], pad], axis=1)]
    reshape x2 -> x3, local copies, waits for them, and re-layouts: 18 us -> 23.4 us  [the longest x1 16.1 us: per_device(): slot_xu.reshape(experts, body, 128)]
  transfers between devices with their start and end apart: 5 -> 4, of which waited for: 4 -> 3; matrix products, arithmetic and copies ran while one was open for 10% -> 10% of each run, Pallas kernels for 0% -> 0%
where the time goes in v4:
time: 514 us; the launch traced here: 512 us
  blocking collectives  272 us (53%)
  local copies, waits for them, and re-layouts  81.5 us (16%)
  waiting for transfers between devices  52.5 us (10%)
  matrix products  42.3 us (8%)
  starting transfers between devices  29.8 us (6%)
  other arithmetic  19.7 us (4%)
  between operations  14.2 us (3%)
    all_to_all x1, blocking collectives, per_device(): lax.all_to_all(packed, 'expert', split_axis=0, concat_axis=0, tiled=True)  201 us
    all_gather x1, blocking collectives, per_device(): lax.all_gather(score.astype(jnp.bfloat16), DP, axis=0, tiled=False)  42.6 us
    all_gather x1, waiting for transfers between devices, per_device(): all_xu = lax.all_gather(recv_xu, 'core', axis=0, tiled=False)  26.4 us
    all_to_all x1, waiting for transfers between devices, per_device(): lax.all_to_all(row_sum.reshape(experts, capacity * part // 128, 128), 'ex...  24.8 us
    all_to_all x1, blocking collectives, per_device(): lax.all_to_all(row_grad.astype(jnp.bfloat16).reshape(n_z, n_c, rows, part...  18.1 us
    reshape x1, local copies, waits for them, and re-layouts, per_device(): slot_xu.reshape(experts, body, 128)  16.1 us
    another operation x1, local copies, waits for them, and re-layouts, per_device(): all_xu = lax.all_gather(recv_xu, 'core', axis=0, tiled=False)  15.5 us
    all_to_all x1, starting transfers between devices, per_device(): lax.all_to_all(score_sum.astype(jnp.bfloat16).reshape(experts, capacity),...  12.3 us
  transfers between devices with their start and end apart: 4, of which 3 were waited for; matrix products, arithmetic and copies ran while one was open for 10% of the time, Pallas kernels for 0%

profile of v4, /device:TPU:1, one launch (start us, length us, event | category | flops | bytes accessed | tf_op | source)
XLA Modules:
  0.0 511.7 jit_solution(11320365854395393640)
XLA Ops:
  10.9 1.5 convert_reduce_fusion
  13.6 5.5 %convolution_convert_fusion = bf16[1152,3584]{1,0:T(8,128)(2,1)} fusion(bf16[128,1792]{1,0:T(8,128)(2,1)S(1)} %get-tuple-element.18, bf16[128,1792]{1,0:T(8,128)(2,1)S(1)} %get-tuple-element.19, bf16[128,1152]{1,0:T(8,128)(2,1)S(1)} %convert_reduce_fusion), kind=kOutput, calls=%fused_computation.7 | convolution fusion | flops 1062928384 | bytes 9469952 | tf_op jit(solution)/shard_map/dot_general | solution.py:73
  19.1 16.1 %reshape.133 = bf16[64,504,128]{2,1,0:T(8,128)(2,1)} reshape(bf16[1152,3584]{1,0:T(8,128)(2,1)} %convolution_convert_fusion) | data formatting | bytes 16515072 | tf_op jit(solution)/shard_map/reshape | solution.py:82
  35.3 4.4 fusion.3
  39.7 201.5 %all_to_all.30 = bf16[64,505,128]{2,1,0:T(8,128)(2,1)} all-to-all(bf16[64,505,128]{2,1,0:T(8,128)(2,1)S(1)} %fusion.3), channel_id=1, replica_groups=mesh['zlo'=2,'core'=2,'expert'=64] {'expert'}, dimensions={0} | all-to-all | bytes 16547840 | tf_op jit(solution)/shard_map/all_to_all | solution.py:87
  241.2 7.1 %slice.18 = bf16[64,504,128]{2,1,0:T(8,128)(2,1)} slice(bf16[64,505,128]{2,1,0:T(8,128)(2,1)} %all_to_all.30), slice={[0:64], [0:504], [0:128]} | slice | bytes 16515072 | tf_op jit(solution)/shard_map/slice | solution.py:89
  248.3 15.5 %all_gather_reshape.3 = bf16[1,1152,3584]{2,1,0:T(8,128)(2,1)} reshape(bf16[64,504,128]{2,1,0:T(8,128)(2,1)} %slice.18) | data formatting | bytes 16515072 | tf_op jit(solution)/shard_map/all_gather;reshape | solution.py:91
  263.8 4.9 reshape_squeeze.11
  269.8 26.4 %all-gather.4.cloned.1.call-done = bf16[2,1152,3584]{2,1,0:T(8,128)(2,1)} async-done(((bf16[1,1152,3584]{2,1,0:T(8,128)(2,1)}), bf16[2,1152,3584]{2,1,0:T(8,128)(2,1)}) %all-gather.4.cloned.1.call-update) | async-done | bytes 16515088 | tf_op jit(solution)/shard_map/all_gather | solution.py:91
  296.2 5.8 %fusion.13 = f32[1152,256]{1,0:T(8,128)S(1)} fusion(bf16[2,1792,256]{2,1,0:T(8,128)(2,1)S(1)} %bitcast.37, bf16[2,1152,3584]{2,1,0:T(8,128)(2,1)} %all-gather.4.cloned.1.call-done), kind=kOutput, calls=%fused_computation.22 | convolution fusion | flops 2113929216 | bytes 11272192 | tf_op jit(solution)/shard_map/hrk,hkf->rf/dot_general | solution.py:33
  302.1 2.8 copy-done.4
  304.8 2.7 fusion.18
  307.5 4.6 convolution_convert_fusion.1
  312.1 7.2 %copy.45 = bf16[2,2,1152,896]{3,2,0,1:T(8,128)(2,1)} copy(bf16[2,2,1152,896]{3,2,1,0:T(8,128)(2,1)} %bitcast.39) | data formatting | bytes 16515072 | tf_op jit(solution)/shard_map/reshape | solution.py:98
  319.2 18.1 %all_to_all.31 = bf16[2,2,1152,896]{3,2,0,1:T(8,128)(2,1)} all-to-all(bf16[2,2,1152,896]{3,2,0,1:T(8,128)(2,1)} %copy.45), channel_id=1, replica_groups=mesh['zlo'=2,'core'=2,'expert'=64] {'core'}, dimensions={1} | all-to-all | bytes 16515072 | tf_op jit(solution)/shard_map/all_to_all | solution.py:97
  337.3 7.8 %reduce_sum.65 = bf16[2,1152,896]{2,1,0:T(8,128)(2,1)} reduce(bf16[2,2,1152,896]{3,2,0,1:T(8,128)(2,1)} %all_to_all.31, bf16[]{:T(256)} %constant.36.clone.1), dimensions={1}, to_apply=%region_2.3 | reduce | flops 2064384 | bytes 12386306 | tf_op jit(solution)/shard_map/reduce_sum | solution.py:100
  345.1 5.9 %all-to-all-start.2 = ((bf16[2,1152,896]{2,1,0:T(8,128)(2,1)}), bf16[2,1152,896]{2,1,0:T(8,128)(2,1)}, u32[]{:S(2)}, u32[]{:S(2)}) async-start(bf16[2,1152,896]{2,1,0:T(8,128)(2,1)} %reduce_sum.65), calls=%async_computation.2 | async-start | bytes 8257536 | tf_op jit(solution)/shard_map/all_to_all | solution.py:101
  351.0 5.5 %fusion.2 = bf16[1152]{0:T(1024)(128)(2,1)S(1)} fusion(bf16[2,1152,3584]{2,1,0:T(8,128)(2,1)} %all-gather.4.cloned.1.call-done, bf16[256,2,1792]{2,1,0:T(2,128)(2,1)S(1)} %copy-done.3, f32[1152,256]{1,0:T(8,128)} %copy-done.5), kind=kOutput, calls=%fused_computation.6 | convolution fusion | flops 2127788928 | bytes 11274496 | tf_op jit(solution)/shard_map/rf,fhk->hrk/dot_general | solution.py:35
  356.6 42.6 %all-gather.1 = bf16[4,1,1152]{2,1,0:T(2,128)(2,1)S(1)} all-gather(bf16[1,1,1152]{2,1,0:T(2,128)(2,1)S(1)} %reshape.150), channel_id=2, replica_groups=mesh['zlo'=2,'core'=2,'expert'=64] {'zlo','core'}, dimensions={0}, use_global_device_ids=true | all-gather | bytes 11520 | tf_op jit(solution)/shard_map/all_gather | solution.py:103
  400.0 12.3 %all-to-all-start.4 = ((bf16[64,1,18]{2,1,0:T(2,128)(2,1)}), bf16[64,1,18]{2,1,0:T(2,128)(2,1)S(1)}, u32[]{:S(2)}, u32[]{:S(2)}) async-start(bf16[64,1,18]{2,1,0:T(2,128)(2,1)} %all_to_all.24), calls=%async_computation.4 | async-start | bytes 65536 | tf_op jit(solution)/shard_map/all_to_all | solution.py:110
  412.4 4.9 reduce_sum.66
  417.2 4.7 reshape.137
  423.1 11.5 %all-to-all-start.3 = ((bf16[64,126,128]{2,1,0:T(8,128)(2,1)}), bf16[64,126,128]{2,1,0:T(8,128)(2,1)}, u32[]{:S(2)}, u32[]{:S(2)}) async-start(bf16[64,126,128]{2,1,0:T(8,128)(2,1)} %reshape.137), calls=%async_computation.3 | async-start | bytes 4194304 | tf_op jit(solution)/shard_map/all_to_all | solution.py:106
  434.8 7.6 %convolution_convert_fusion.2 = bf16[256,2,1792]{2,0,1:T(8,128)(2,1)} fusion(f32[1152]{0:T(1024)S(1)} %reshape.139, bf16[2,1152,3584]{2,1,0:T(8,128)(2,1)} %all-gather.4.cloned.1.call-done, f32[1152,256]{1,0:T(8,128)S(1)} %copy-done.6), kind=kOutput, calls=%fused_computation.21 | convolution fusion | flops 2128707584 | bytes 11276800 | tf_op jit(solution)/shard_map/rf,hrk->fhk/dot_general | solution.py:43
  442.3 2.8 copy.50
  445.1 2.6 copy.52
  447.7 7.2 %fusion.10 = bf16[2,1792,256]{2,1,0:T(8,128)(2,1)} fusion(bf16[1152,256,1]{1,0,2:T(8,128)(2,1)S(1)} %fusion.18, bf16[2,1152,3584]{2,1,0:T(8,128)(2,1)} %all-gather.4.cloned.1.call-done), kind=kOutput, calls=%fused_computation.20 | convolution fusion | flops 2114846720 | bytes 10682368 | tf_op jit(solution)/shard_map/hrk,rf->hkf/dot_general | solution.py:44
  455.1 6.8 %gather_fusion = bf16[1024]{0:T(1024)(128)(2,1)S(1)} fusion(bf16[1152]{0:T(1024)(128)(2,1)S(1)} %reshape.140, s32[1024]{0:T(1024)S(1)} %broadcast_clamp_fusion), kind=kCustom, calls=%fused_computation | custom fusion | bytes 8192 | tf_op jit(solution)/shard_map/jit(_take)/gather | solution.py:120
  462.7 24.8 %all-to-all-done.3 = bf16[64,126,128]{2,1,0:T(8,128)(2,1)} async-done(((bf16[64,126,128]{2,1,0:T(8,128)(2,1)}), bf16[64,126,128]{2,1,0:T(8,128)(2,1)}, u32[]{:S(2)}, u32[]{:S(2)}) %all-to-all-start.3) | async-done | bytes 2064416 | tf_op jit(solution)/shard_map/all_to_all | solution.py:106
  487.6 4.9 reshape.138
  492.4 2.1 convolution_convert_fusion.3
  494.5 9.4 %all_gather.11 = bf16[128,3584]{1,0:T(8,128)(2,1)S(1)} all-gather(bf16[128,896]{1,0:T(8,128)(2,1)S(1)} %convolution_convert_fusion.3), channel_id=1, replica_groups=mesh['zlo'=2,'core'=2,'expert'=64] {'zlo','core'}, dimensions={1}, use_global_device_ids=true | all-gather | bytes 1146880 | tf_op jit(solution)/shard_map/all_gather | solution.py:118
  (43 shorter events, 10.2 us)
Async XLA Ops:
  7.2 289.1 %copy-start = (bf16[1,3584,256]{2,1,0:T(8,128)(2,1)S(1)}, bf16[1,3584,256]{2,1,0:T(8,128)(2,1)}, u32[]{:S(2)}) copy-start(bf16[1,3584,256]{2,1,0:T(8,128)(2,1)} %param.10) | copy-start | bytes 5505028
  7.2 289.0 %all-gather.4.cloned.1.call-start = ((), (), s32[]{:S(2)}) async-start(), calls=%async_computation.5 | async-start | bytes 24772608 | tf_op jit(solution)/shard_map/all_gather | solution.py:91
  296.2 5.8 %copy-start.2 = (bf16[256,2,1792]{2,1,0:T(2,128)(2,1)S(1)}, bf16[256,2,1792]{2,1,0:T(2,128)(2,1)}, u32[]{:S(2)}) copy-start(bf16[256,2,1792]{2,1,0:T(2,128)(2,1)} %reshape_squeeze.11) | copy-start | bytes 5505028
  296.2 8.6 %copy-start.4 = (bf16[2,1152,3584]{2,1,0:T(8,128)(2,1)S(1)}, bf16[2,1152,3584]{2,1,0:T(8,128)(2,1)}, u32[]{:S(2)}) copy-start(bf16[2,1152,3584]{2,1,0:T(8,128)(2,1)} %all-gather.4.cloned.1.call-done) | copy-start | bytes 49545220
  304.8 2.7 copy-start.5
  345.1 5.9 %copy-start.3 = (bf16[256,2,1792]{2,1,0:T(2,128)(2,1)S(1)}, bf16[256,2,1792]{2,1,0:T(2,128)(2,1)}, u32[]{:S(2)}) copy-start(bf16[256,2,1792]{2,1,0:T(2,128)(2,1)} %reshape_squeeze.11) | copy-start | bytes 5505028
  345.1 54.9 %all-to-all-start.2 = ((bf16[2,1152,896]{2,1,0:T(8,128)(2,1)}), bf16[2,1152,896]{2,1,0:T(8,128)(2,1)}, u32[]{:S(2)}, u32[]{:S(2)}) async-start(bf16[2,1152,896]{2,1,0:T(8,128)(2,1)} %reduce_sum.65), calls=%async_computation.2 | async-start | bytes 8257536 | tf_op jit(solution)/shard_map/all_to_all | solution.py:101
  400.0 23.1 %all-to-all-start.4 = ((bf16[64,1,18]{2,1,0:T(2,128)(2,1)}), bf16[64,1,18]{2,1,0:T(2,128)(2,1)S(1)}, u32[]{:S(2)}, u32[]{:S(2)}) async-start(bf16[64,1,18]{2,1,0:T(2,128)(2,1)} %all_to_all.24), calls=%async_computation.4 | async-start | bytes 65536 | tf_op jit(solution)/shard_map/all_to_all | solution.py:110
  417.2 17.6 %copy-start.6 = (f32[1152,256]{1,0:T(8,128)S(1)}, f32[1152,256]{1,0:T(8,128)}, u32[]{:S(2)}) copy-start(f32[1152,256]{1,0:T(8,128)} %copy-done.5) | copy-start | bytes 3538948
  423.1 64.4 %all-to-all-start.3 = ((bf16[64,126,128]{2,1,0:T(8,128)(2,1)}), bf16[64,126,128]{2,1,0:T(8,128)(2,1)}, u32[]{:S(2)}, u32[]{:S(2)}) async-start(bf16[64,126,128]{2,1,0:T(8,128)(2,1)} %reshape.137), calls=%async_computation.3 | async-start | bytes 4194304 | tf_op jit(solution)/shard_map/all_to_all | solution.py:106
  487.5 17.3 %copy-start.1 = (bf16[1,3584,256]{2,1,0:T(8,128)(2,1)S(1)}, bf16[1,3584,256]{2,1,0:T(8,128)(2,1)}, u32[]{:S(2)}) copy-start(bf16[1,3584,256]{2,1,0:T(8,128)(2,1)} %param.10) | copy-start | bytes 5505028
Sparse Core Ops, SparseCore 0:
  263.9 32.3 all-gather.3

commit v5 on v4

--- a/solution.py
+++ b/solution.py
@@ -94,24 +94,32 @@
     row_grad, score, grad_in, grad_out = expert_terms(
         all_x, all_u, recv_p, block_in, block_out, n_z * n_c
     )
-    on_chip = lax.all_to_all(
-        row_grad.astype(jnp.bfloat16).reshape(n_z, n_c, rows, part), "core", split_axis=1, concat_axis=1, tiled=True
+    rg = row_grad.astype(jnp.bfloat16).reshape(n_z, n_c, rows, part)
+    nrow = -(-rows // part)
+    srow = jnp.pad(score.astype(jnp.bfloat16), (0, nrow * part - rows)).reshape(1, 1, nrow, part)
+    chunk = jnp.concatenate([rg, jnp.broadcast_to(srow, (n_z, n_c, nrow, part))], axis=2)
+    on_chip = lax.all_to_all(chunk, "core", split_axis=1, concat_axis=1, tiled=True)
+    chip_sum = jnp.sum(on_chip[:, :, :rows].astype(jnp.float32), axis=1).astype(jnp.bfloat16)
+    chip_scores = on_chip[:, :, rows:].reshape(n_z, n_c * nrow, part)
+    chunk2 = jnp.concatenate([chip_sum, chip_scores], axis=1)
+    off_chip = lax.all_to_all(chunk2, "zlo", split_axis=0, concat_axis=0, tiled=True)
+    row_sum = jnp.sum(off_chip[:, :rows].astype(jnp.float32), axis=0).astype(jnp.bfloat16)
+    block_scores = off_chip[:, rows:].reshape(n_z * n_c, nrow * part)[:, :rows]
+    score_sum = jnp.sum(block_scores.astype(jnp.float32), axis=0)
+    body2 = capacity * part // 128
+    packed2 = jnp.concatenate(
+        [
+            row_sum.reshape(experts, body2, 128),
+            jnp.pad(
+                score_sum.astype(jnp.bfloat16).reshape(experts, 1, capacity),
+                ((0, 0), (0, 0), (0, 128 - capacity)),
+            ),
+        ],
+        axis=1,
     )
-    chip_sum = jnp.sum(on_chip.astype(jnp.float32), axis=1).astype(jnp.bfloat16)
-    off_chip = lax.all_to_all(chip_sum, "zlo", split_axis=0, concat_axis=0, tiled=True)
-    row_sum = jnp.sum(off_chip.astype(jnp.float32), axis=0).astype(jnp.bfloat16)
-    score_all = lax.all_gather(score.astype(jnp.bfloat16), DP, axis=0, tiled=False)
-    score_sum = jnp.sum(score_all.astype(jnp.float32), axis=0)
-    back_x, back_s = (
-        lax.all_to_all(
-            row_sum.reshape(experts, capacity * part // 128, 128), "expert", split_axis=0,
-            concat_axis=0, tiled=True,
-        ),
-        lax.all_to_all(
-            score_sum.astype(jnp.bfloat16).reshape(experts, capacity), "expert", split_axis=0,
-            concat_axis=0, tiled=True,
-        ),
-    )
+    back = lax.all_to_all(packed2, "expert", split_axis=0, concat_axis=0, tiled=True)
+    back_x = back[:, :body2, :]
+    back_s = back[:, body2, :capacity]
     token_part = jnp.dot(
         pick, back_x.reshape(experts * capacity, part), preferred_element_type=jnp.float32
     )

time: 514 us -> 621 us (1.21)
  local copies, waits for them, and re-layouts: 81.5 us -> 156 us
  other arithmetic: 19.7 us -> 59.2 us
  starting transfers between devices: 29.8 us -> 12.9 us
    reshape x2 -> x4, local copies, waits for them, and re-layouts: 11.9 us -> 84.5 us  [the longest x1 79.6 us: per_device(): rg = row_grad.astype(jnp.bfloat16).reshape(n_z, n_c, rows, part)]
    all_gather x1 -> x0, blocking collectives: 42.6 us -> none  [per_device(): lax.all_gather(score.astype(jnp.bfloat16), DP, axis=0, tiled=False)]
    all_to_all x1 -> x2, blocking collectives: 18.1 us -> 59.7 us  [the longest x1 49.3 us: per_device(): lax.all_to_all(chunk2, 'zlo', split_axis=0, concat_axis=0, tiled=True)]
    concatenate x0 -> x3, other arithmetic: none -> 32.8 us  [the longest x1 19.6 us: per_device(): jnp.concatenate([rg, jnp.broadcast_to(srow, (n_z, n_c, nrow, part))], axi...]
    all_to_all x3 -> x1, starting transfers between devices: 29.8 us -> 12.8 us  [per_device(): lax.all_to_all(packed2, 'expert', split_axis=0, concat_axis=0, tiled=True)]
    all_to_all x3 -> x1, waiting for transfers between devices: 26 us -> 32.6 us  [per_device(): lax.all_to_all(packed2, 'expert', split_axis=0, concat_axis=0, tiled=True)]
  transfers between devices with their start and end apart: 4 -> 2, of which waited for: 3 -> 2; matrix products, arithmetic and copies ran while one was open for 10% -> 4% of each run, Pallas kernels for 0% -> 0%
where the time goes in v5:
time: 621 us; the launch traced here: 614 us
  blocking collectives  271 us (44%)
  local copies, waits for them, and re-layouts  156 us (25%)
  other arithmetic  59.2 us (10%)
  waiting for transfers between devices  58.3 us (9%)
  matrix products  41.7 us (7%)
  between operations  14.8 us (2%)
  starting transfers between devices  12.9 us (2%)
    all_to_all x1, blocking collectives, per_device(): lax.all_to_all(packed, 'expert', split_axis=0, concat_axis=0, tiled=True)  202 us
    reshape x1, local copies, waits for them, and re-layouts, per_device(): rg = row_grad.astype(jnp.bfloat16).reshape(n_z, n_c, rows, part)  79.6 us
    all_to_all x1, blocking collectives, per_device(): lax.all_to_all(chunk2, 'zlo', split_axis=0, concat_axis=0, tiled=True)  49.3 us
    all_to_all x1, waiting for transfers between devices, per_device(): lax.all_to_all(packed2, 'expert', split_axis=0, concat_axis=0, tiled=True)  32.6 us
    all_gather x1, waiting for transfers between devices, per_device(): all_xu = lax.all_gather(recv_xu, 'core', axis=0, tiled=False)  25.8 us
    concatenate x1, other arithmetic, per_device(): jnp.concatenate([rg, jnp.broadcast_to(srow, (n_z, n_c, nrow, part))], axi...  19.6 us
    reshape x1, local copies, waits for them, and re-layouts, per_device(): slot_xu.reshape(experts, body, 128)  16.1 us
    another operation x1, local copies, waits for them, and re-layouts, per_device(): all_xu = lax.all_gather(recv_xu, 'core', axis=0, tiled=False)  15.5 us
  transfers between devices with their start and end apart: 2, of which 2 were waited for; matrix products, arithmetic and copies ran while one was open for 4% of the time, Pallas kernels for 0%

profile of v5, /device:TPU:1, one launch (start us, length us, event | category | flops | bytes accessed | tf_op | source)
XLA Modules:
  0.0 614.1 jit_solution(13452456695942677866)
XLA Ops:
  13.6 5.5 convolution_convert_fusion
  19.1 16.1 %reshape.130 = bf16[64,504,128]{2,1,0:T(8,128)(2,1)} reshape(bf16[1152,3584]{1,0:T(8,128)(2,1)} %convolution_convert_fusion) | data formatting | bytes 16515072 | tf_op jit(solution)/shard_map/reshape | solution.py:82
  35.2 4.4 fusion.3
  39.7 202.2 %all_to_all.20 = bf16[64,505,128]{2,1,0:T(8,128)(2,1)} all-to-all(bf16[64,505,128]{2,1,0:T(8,128)(2,1)S(1)} %fusion.3), channel_id=1, replica_groups=mesh['zlo'=2,'core'=2,'expert'=64] {'expert'}, dimensions={0} | all-to-all | bytes 16547840 | tf_op jit(solution)/shard_map/all_to_all | solution.py:87
  241.8 7.1 %slice.46 = bf16[64,504,128]{2,1,0:T(8,128)(2,1)} slice(bf16[64,505,128]{2,1,0:T(8,128)(2,1)} %all_to_all.20), slice={[0:64], [0:504], [0:128]} | slice | bytes 16515072 | tf_op jit(solution)/shard_map/slice | solution.py:89
  248.9 15.5 %all_gather_reshape.3 = bf16[1,1152,3584]{2,1,0:T(8,128)(2,1)} reshape(bf16[64,504,128]{2,1,0:T(8,128)(2,1)} %slice.46) | data formatting | bytes 16515072 | tf_op jit(solution)/shard_map/all_gather;reshape | solution.py:91
  264.4 4.9 reshape_squeeze.12
  270.4 25.8 %all-gather.2.cloned.1.call-done = bf16[2,1152,3584]{2,1,0:T(8,128)(2,1)} async-done(((bf16[1,1152,3584]{2,1,0:T(8,128)(2,1)}), bf16[2,1152,3584]{2,1,0:T(8,128)(2,1)}) %all-gather.2.cloned.1.call-update) | async-done | bytes 16515088 | tf_op jit(solution)/shard_map/all_gather | solution.py:91
  296.2 5.8 fusion.14
  302.1 2.7 copy-done.11
  304.8 3.1 fusion.2
  308.0 6.4 %fusion.19 = bf16[1152,256,1]{1,0,2:T(8,128)(2,1)S(1)} fusion(f32[1152]{0:T(1024)S(1)} %reshape.139, bf16[2,1152,3584]{2,1,0:T(8,128)(2,1)} %all-gather.2.cloned.1.call-done, bf16[256,2,1792]{2,1,0:T(2,128)(2,1)} %reshape_squeeze.12, f32[1152,256]{1,0:T(8,128)S(1)} %fusion.14), kind=kOutput, calls=%fused_computation.32 | convolution fusion | flops 2128969728 | bytes 11866624 | tf_op jit(solution)/shard_map/hrk,fhk->rf/dot_general | solution.py:40
  314.4 2.6 convolution_convert_fusion.1
  317.0 79.6 %copy.89 = bf16[2,2,1152,896]{3,0,2,1:T(2,128)(2,1)S(1)} copy(bf16[2,2,1152,896]{3,2,1,0:T(8,128)(2,1)S(1)} %bitcast.41) | data formatting | bytes 16515072 | tf_op jit(solution)/shard_map/reshape | solution.py:97
  396.7 19.6 %pad_maximum_fusion = bf16[2,2,1154,896]{3,0,2,1:T(2,128)(2,1)S(1)} fusion(bf16[2,2,2,896]{3,0,2,1:T(2,128)(2,1)S(1)} %broadcast_in_dim.16, bf16[2,2,1152,896]{3,0,2,1:T(2,128)(2,1)S(1)} %copy.89), kind=kLoop, calls=%fused_computation.10 | loop fusion | flops 4135936 | bytes 16543744 | tf_op jit(solution)/shard_map/concatenate | solution.py:100
  416.3 10.4 %all_to_all.21 = bf16[2,2,1154,896]{3,0,2,1:T(2,128)(2,1)S(1)} all-to-all(bf16[2,2,1154,896]{3,0,2,1:T(2,128)(2,1)S(1)} %pad_maximum_fusion), channel_id=1, replica_groups=mesh['zlo'=2,'core'=2,'expert'=64] {'core'}, dimensions={1} | all-to-all | bytes 16543744 | tf_op jit(solution)/shard_map/all_to_all | solution.py:101
  426.7 13.6 %slice_reduce_fusion = bf16[2,1152,896]{2,0,1:T(2,128)(2,1)S(1)} fusion(bf16[2,2,1154,896]{3,0,2,1:T(2,128)(2,1)S(1)} %all_to_all.21), kind=kLoop, calls=%fused_computation.11 | loop fusion | flops 2064384 | bytes 12386304 | tf_op jit(solution)/shard_map/reduce_sum | solution.py:102
  440.3 9.8 %pad_maximum_fusion.1 = bf16[2,1156,896]{2,0,1:T(2,128)(2,1)S(1)} fusion(bf16[2,4,896]{2,0,1:T(2,128)(2,1)S(1)} %bitcast.43, bf16[2,1152,896]{2,0,1:T(2,128)(2,1)S(1)} %slice_reduce_fusion), kind=kLoop, calls=%fused_computation.24 | loop fusion | flops 2071552 | bytes 8286208 | tf_op jit(solution)/shard_map/concatenate | solution.py:104
  450.6 49.3 %all_to_all.22 = bf16[2,1156,896]{2,1,0:T(8,128)(2,1)S(1)} all-to-all(bf16[2,1156,896]{2,1,0:T(8,128)(2,1)S(1)} %copy.90), channel_id=1, replica_groups=mesh['zlo'=2,'core'=2,'expert'=64] {'zlo'}, dimensions={0} | all-to-all | bytes 8286208 | tf_op jit(solution)/shard_map/all_to_all | solution.py:105
  502.1 4.8 slice_reduce_fusion.1
  507.0 4.7 reshape.135
  511.6 3.4 fusion.23
  515.0 12.8 %all-to-all-start.3 = ((bf16[64,127,128]{2,1,0:T(8,128)(2,1)}), bf16[64,127,128]{2,1,0:T(8,128)(2,1)}, u32[]{:S(2)}, u32[]{:S(2)}) async-start(bf16[64,127,128]{2,1,0:T(8,128)(2,1)} %fusion.23), calls=%async_computation.3 | async-start | bytes 4194304 | tf_op jit(solution)/shard_map/all_to_all | solution.py:120
  528.0 7.5 %convolution_convert_fusion.2 = bf16[256,2,1792]{2,0,1:T(8,128)(2,1)} fusion(f32[1152]{0:T(1024)S(1)} %copy-done.10, bf16[2,1152,3584]{2,1,0:T(8,128)(2,1)} %all-gather.2.cloned.1.call-done, f32[1152,256]{1,0:T(8,128)S(1)} %copy-done.13), kind=kOutput, calls=%fused_computation.27 | convolution fusion | flops 2128707584 | bytes 11276800 | tf_op jit(solution)/shard_map/rf,hrk->fhk/dot_general | solution.py:43
  535.5 2.9 copy.94
  538.4 2.6 copy.96
  541.0 7.2 %fusion.11 = bf16[2,1792,256]{2,1,0:T(8,128)(2,1)} fusion(bf16[1152,256,1]{1,0,2:T(8,128)(2,1)S(1)} %copy-done.5, bf16[2,1152,3584]{2,1,0:T(8,128)(2,1)} %all-gather.2.cloned.1.call-done), kind=kOutput, calls=%fused_computation.26 | convolution fusion | flops 2114846720 | bytes 10682368 | tf_op jit(solution)/shard_map/hrk,rf->hkf/dot_general | solution.py:44
  548.2 32.6 %all-to-all-done.3 = bf16[64,127,128]{2,1,0:T(8,128)(2,1)} async-done(((bf16[64,127,128]{2,1,0:T(8,128)(2,1)}), bf16[64,127,128]{2,1,0:T(8,128)(2,1)}, u32[]{:S(2)}, u32[]{:S(2)}) %all-to-all-start.3) | async-done | bytes 2080800 | tf_op jit(solution)/shard_map/all_to_all | solution.py:120
  581.9 6.8 %gather_fusion = bf16[1024]{0:T(1024)(128)(2,1)S(1)} fusion(bf16[1152]{0:T(1024)(128)(2,1)S(1)} %reshape.140, s32[1024]{0:T(1024)S(1)} %broadcast_clamp_fusion), kind=kCustom, calls=%fused_computation | custom fusion | bytes 8192 | tf_op jit(solution)/shard_map/jit(_take)/gather | solution.py:128
  589.5 4.9 reshape.138
  594.3 2.1 convolution_convert_fusion.3
  596.4 9.4 %all_gather.7 = bf16[128,3584]{1,0:T(8,128)(2,1)S(1)} all-gather(bf16[128,896]{1,0:T(8,128)(2,1)S(1)} %convolution_convert_fusion.3), channel_id=1, replica_groups=mesh['zlo'=2,'core'=2,'expert'=64] {'zlo','core'}, dimensions={1}, use_global_device_ids=true | all-gather | bytes 1146880 | tf_op jit(solution)/shard_map/all_gather | solution.py:126
  (62 shorter events, 13.2 us)
Async XLA Ops:
  7.2 289.0 %copy-start = (bf16[1,3584,256]{2,1,0:T(8,128)(2,1)S(1)}, bf16[1,3584,256]{2,1,0:T(8,128)(2,1)}, u32[]{:S(2)}) copy-start(bf16[1,3584,256]{2,1,0:T(8,128)(2,1)} %param.10) | copy-start | bytes 5505028
  7.2 5.3 copy-start.6
  7.2 289.0 %all-gather.2.cloned.1.call-start = ((), (), s32[]{:S(2)}) async-start(), calls=%async_computation.4 | async-start | bytes 24772608 | tf_op jit(solution)/shard_map/all_gather | solution.py:91
  8.9 10.2 %copy-start.7 = (s32[1024]{0:T(1024)}, s32[1024]{0:T(1024)S(1)}, u32[]{:S(2)}) copy-start(s32[1024]{0:T(1024)S(1)} %convert_element_type.120) | copy-start | bytes 12292
  270.4 37.5 %copy-start.9 = (f32[1152]{0:T(1024)}, f32[1152]{0:T(1024)S(1)}, u32[]{:S(2)}) copy-start(f32[1152]{0:T(1024)S(1)} %reshape.139) | copy-start | bytes 13828
  296.2 5.9 copy-start.3
  296.2 8.6 %copy-start.11 = (bf16[2,1152,3584]{2,1,0:T(8,128)(2,1)S(1)}, bf16[2,1152,3584]{2,1,0:T(8,128)(2,1)}, u32[]{:S(2)}) copy-start(bf16[2,1152,3584]{2,1,0:T(8,128)(2,1)} %all-gather.2.cloned.1.call-done) | copy-start | bytes 49545220
  304.8 3.2 copy-start.12
  314.4 2.6 copy-start.4
  499.9 2.0 copy-start.2
  511.6 16.4 %copy-start.8 = (s32[1024]{0:T(1024)S(1)}, s32[1024]{0:T(1024)}, u32[]{:S(2)}) copy-start(s32[1024]{0:T(1024)} %copy-done.7) | copy-start | bytes 12292
  511.6 16.4 %copy-start.10 = (f32[1152]{0:T(1024)S(1)}, f32[1152]{0:T(1024)}, u32[]{:S(2)}) copy-start(f32[1152]{0:T(1024)} %copy-done.9) | copy-start | bytes 13828
  511.6 16.4 %copy-start.13 = (f32[1152,256]{1,0:T(8,128)S(1)}, f32[1152,256]{1,0:T(8,128)}, u32[]{:S(2)}) copy-start(f32[1152,256]{1,0:T(8,128)} %copy-done.12) | copy-start | bytes 3538948
  515.0 65.7 %all-to-all-start.3 = ((bf16[64,127,128]{2,1,0:T(8,128)(2,1)}), bf16[64,127,128]{2,1,0:T(8,128)(2,1)}, u32[]{:S(2)}, u32[]{:S(2)}) async-start(bf16[64,127,128]{2,1,0:T(8,128)(2,1)} %fusion.23), calls=%async_computation.3 | async-start | bytes 4194304 | tf_op jit(solution)/shard_map/all_to_all | solution.py:120
  535.5 5.4 copy-start.5
  589.5 17.3 %copy-start.1 = (bf16[1,3584,256]{2,1,0:T(8,128)(2,1)S(1)}, bf16[1,3584,256]{2,1,0:T(8,128)(2,1)}, u32[]{:S(2)}) copy-start(bf16[1,3584,256]{2,1,0:T(8,128)(2,1)} %param.10) | copy-start | bytes 5505028
Sparse Core Ops, SparseCore 0:
  264.5 31.6 all-gather.1

commit v6 on v5

--- a/solution.py
+++ b/solution.py
@@ -95,7 +95,7 @@
         all_x, all_u, recv_p, block_in, block_out, n_z * n_c
     )
     rg = row_grad.astype(jnp.bfloat16).reshape(n_z, n_c, rows, part)
-    nrow = -(-rows // part)
+    nrow = -(-rows // (16 * part)) * 16
     srow = jnp.pad(score.astype(jnp.bfloat16), (0, nrow * part - rows)).reshape(1, 1, nrow, part)
     chunk = jnp.concatenate([rg, jnp.broadcast_to(srow, (n_z, n_c, nrow, part))], axis=2)
     on_chip = lax.all_to_all(chunk, "core", split_axis=1, concat_axis=1, tiled=True)

time: 621 us -> 502 us (0.81)
  local copies, waits for them, and re-layouts: 156 us -> 79 us
  other arithmetic: 59.2 us -> 21.9 us
    reshape x1 -> x0, local copies, waits for them, and re-layouts: 79.6 us -> none  [per_device(): rg = row_grad.astype(jnp.bfloat16).reshape(n_z, n_c, rows, part)]
    concatenate x1, other arithmetic: 19.6 us -> 0.76 us  [per_device(): jnp.concatenate([rg, jnp.broadcast_to(srow, (n_z, n_c, nrow, part))], axi...]
    concatenate x1, other arithmetic: 9.79 us -> 0.34 us  [per_device(): chunk2 = jnp.concatenate([chip_sum, chip_scores], axis=1)]
    reduce_sum x1, other arithmetic: 13.6 us -> 4.54 us  [per_device(): jnp.sum(on_chip[:, :, :rows].astype(jnp.float32), axis=1)]
    unnamed x33 -> x26, local copies, waits for them, and re-layouts: 10.7 us -> 13.9 us
  transfers between devices with their start and end apart: 2 -> 2, of which waited for: 2 -> 2; matrix products, arithmetic and copies ran while one was open for 4% -> 5% of each run, Pallas kernels for 0% -> 0%
where the time goes in v6:
time: 502 us; the launch traced here: 500 us
  blocking collectives  273 us (54%)
  local copies, waits for them, and re-layouts  79 us (16%)
  waiting for transfers between devices  57.2 us (11%)
  matrix products  42 us (8%)
  other arithmetic  21.9 us (4%)
  between operations  14.3 us (3%)
  starting transfers between devices  12.6 us (3%)
    all_to_all x1, blocking collectives, per_device(): lax.all_to_all(packed, 'expert', split_axis=0, concat_axis=0, tiled=True)  203 us
    all_to_all x1, blocking collectives, per_device(): lax.all_to_all(chunk2, 'zlo', split_axis=0, concat_axis=0, tiled=True)  50.3 us
    all_to_all x1, waiting for transfers between devices, per_device(): lax.all_to_all(packed2, 'expert', split_axis=0, concat_axis=0, tiled=True)  31.9 us
    all_gather x1, waiting for transfers between devices, per_device(): all_xu = lax.all_gather(recv_xu, 'core', axis=0, tiled=False)  25.3 us
    reshape x1, local copies, waits for them, and re-layouts, per_device(): slot_xu.reshape(experts, body, 128)  16.1 us
    another operation x1, local copies, waits for them, and re-layouts, per_device(): all_xu = lax.all_gather(recv_xu, 'core', axis=0, tiled=False)  15.5 us
    unnamed x26, local copies, waits for them, and re-layouts  13.9 us
    all_to_all x1, starting transfers between devices, per_device(): lax.all_to_all(packed2, 'expert', split_axis=0, concat_axis=0, tiled=True)  12.6 us
  transfers between devices with their start and end apart: 2, of which 2 were waited for; matrix products, arithmetic and copies ran while one was open for 5% of the time, Pallas kernels for 0%

profile of v6, /device:TPU:1, one launch (start us, length us, event | category | flops | bytes accessed | tf_op | source)
XLA Modules:
  0.0 500.1 jit_solution(50567529434221210)
XLA Ops:
  10.9 1.5 convert_reduce_fusion
  13.6 5.5 %convolution_convert_fusion = bf16[1152,3584]{1,0:T(8,128)(2,1)} fusion(bf16[128,1792]{1,0:T(8,128)(2,1)S(1)} %get-tuple-element.22, bf16[128,1792]{1,0:T(8,128)(2,1)S(1)} %get-tuple-element.23, bf16[128,1152]{1,0:T(8,128)(2,1)S(1)} %convert_reduce_fusion), kind=kOutput, calls=%fused_computation.7 | convolution fusion | flops 1062928384 | bytes 9469952 | tf_op jit(solution)/shard_map/dot_general | solution.py:73
  19.2 16.1 %reshape.130 = bf16[64,504,128]{2,1,0:T(8,128)(2,1)} reshape(bf16[1152,3584]{1,0:T(8,128)(2,1)} %convolution_convert_fusion) | data formatting | bytes 16515072 | tf_op jit(solution)/shard_map/reshape | solution.py:82
  35.3 4.4 fusion.3
  39.7 202.6 %all_to_all.20 = bf16[64,505,128]{2,1,0:T(8,128)(2,1)} all-to-all(bf16[64,505,128]{2,1,0:T(8,128)(2,1)S(1)} %fusion.3), channel_id=1, replica_groups=mesh['zlo'=2,'core'=2,'expert'=64] {'expert'}, dimensions={0} | all-to-all | bytes 16547840 | tf_op jit(solution)/shard_map/all_to_all | solution.py:87
  242.4 7.1 %slice.46 = bf16[64,504,128]{2,1,0:T(8,128)(2,1)} slice(bf16[64,505,128]{2,1,0:T(8,128)(2,1)} %all_to_all.20), slice={[0:64], [0:504], [0:128]} | slice | bytes 16515072 | tf_op jit(solution)/shard_map/slice | solution.py:89
  249.4 15.5 %all_gather_reshape.3 = bf16[1,1152,3584]{2,1,0:T(8,128)(2,1)} reshape(bf16[64,504,128]{2,1,0:T(8,128)(2,1)} %slice.46) | data formatting | bytes 16515072 | tf_op jit(solution)/shard_map/all_gather;reshape | solution.py:91
  264.9 4.9 reshape_squeeze.12
  270.9 25.3 %all-gather.2.cloned.1.call-done = bf16[2,1152,3584]{2,1,0:T(8,128)(2,1)} async-done(((bf16[1,1152,3584]{2,1,0:T(8,128)(2,1)}), bf16[2,1152,3584]{2,1,0:T(8,128)(2,1)}) %all-gather.2.cloned.1.call-update) | async-done | bytes 16515088 | tf_op jit(solution)/shard_map/all_gather | solution.py:91
  296.2 5.8 %fusion.14 = f32[1152,256]{1,0:T(8,128)S(1)} fusion(bf16[2,1792,256]{2,1,0:T(8,128)(2,1)S(1)} %bitcast.39, bf16[2,1152,3584]{2,1,0:T(8,128)(2,1)} %all-gather.2.cloned.1.call-done), kind=kOutput, calls=%fused_computation.28 | convolution fusion | flops 2113929216 | bytes 11272192 | tf_op jit(solution)/shard_map/hrk,hkf->rf/dot_general | solution.py:33
  302.0 2.8 copy-done.7
  304.8 3.1 fusion.2
  308.0 6.8 %fusion.19 = bf16[1152,256,1]{1,0,2:T(8,128)(2,1)S(1)} fusion(f32[1152]{0:T(1024)S(1)} %reshape.139, bf16[2,1152,3584]{2,1,0:T(8,128)(2,1)} %all-gather.2.cloned.1.call-done, bf16[256,2,1792]{2,1,0:T(2,128)(2,1)} %reshape_squeeze.12, f32[1152,256]{1,0:T(8,128)} %copy-done.8), kind=kOutput, calls=%fused_computation.32 | convolution fusion | flops 2128969728 | bytes 11866624 | tf_op jit(solution)/shard_map/hrk,fhk->rf/dot_general | solution.py:40
  314.8 2.6 convolution_convert_fusion.1
  318.2 10.3 %all_to_all.21 = bf16[2,2,1168,896]{3,2,0,1:T(8,128)(2,1)S(1)} all-to-all(bf16[2,2,1168,896]{3,2,0,1:T(8,128)(2,1)S(1)} %pad_maximum_fusion), channel_id=1, replica_groups=mesh['zlo'=2,'core'=2,'expert'=64] {'core'}, dimensions={1} | all-to-all | bytes 16744448 | tf_op jit(solution)/shard_map/all_to_all | solution.py:101
  328.5 3.2 copy-done.2
  331.7 4.5 slice_reduce_fusion
  336.6 50.3 %all_to_all.22 = bf16[2,1184,896]{2,1,0:T(8,128)(2,1)S(1)} all-to-all(bf16[2,1184,896]{2,1,0:T(8,128)(2,1)S(1)} %pad_maximum_fusion.1), channel_id=1, replica_groups=mesh['zlo'=2,'core'=2,'expert'=64] {'zlo'}, dimensions={0} | all-to-all | bytes 8486912 | tf_op jit(solution)/shard_map/all_to_all | solution.py:105
  386.9 2.0 copy-done.3
  389.1 4.9 slice_reduce_fusion.1
  393.9 4.7 reshape.135
  398.6 3.4 fusion.23
  402.0 12.6 %all-to-all-start.3 = ((bf16[64,127,128]{2,1,0:T(8,128)(2,1)}), bf16[64,127,128]{2,1,0:T(8,128)(2,1)}, u32[]{:S(2)}, u32[]{:S(2)}) async-start(bf16[64,127,128]{2,1,0:T(8,128)(2,1)} %fusion.23), calls=%async_computation.3 | async-start | bytes 4194304 | tf_op jit(solution)/shard_map/all_to_all | solution.py:120
  414.8 7.5 %convolution_convert_fusion.2 = bf16[256,2,1792]{2,0,1:T(8,128)(2,1)} fusion(f32[1152]{0:T(1024)S(1)} %reshape.139, bf16[2,1152,3584]{2,1,0:T(8,128)(2,1)} %all-gather.2.cloned.1.call-done, f32[1152,256]{1,0:T(8,128)S(1)} %copy-done.9), kind=kOutput, calls=%fused_computation.27 | convolution fusion | flops 2128707584 | bytes 11276800 | tf_op jit(solution)/shard_map/rf,hrk->fhk/dot_general | solution.py:43
  422.3 2.9 copy.66
  425.1 2.6 copy.68
  427.7 7.2 %fusion.11 = bf16[2,1792,256]{2,1,0:T(8,128)(2,1)} fusion(bf16[1152,256,1]{1,0,2:T(8,128)(2,1)S(1)} %copy-done.6, bf16[2,1152,3584]{2,1,0:T(8,128)(2,1)} %all-gather.2.cloned.1.call-done), kind=kOutput, calls=%fused_computation.26 | convolution fusion | flops 2114846720 | bytes 10682368 | tf_op jit(solution)/shard_map/hrk,rf->hkf/dot_general | solution.py:44
  434.9 31.9 %all-to-all-done.3 = bf16[64,127,128]{2,1,0:T(8,128)(2,1)} async-done(((bf16[64,127,128]{2,1,0:T(8,128)(2,1)}), bf16[64,127,128]{2,1,0:T(8,128)(2,1)}, u32[]{:S(2)}, u32[]{:S(2)}) %all-to-all-start.3) | async-done | bytes 2080800 | tf_op jit(solution)/shard_map/all_to_all | solution.py:120
  467.9 6.8 %gather_fusion = bf16[1024]{0:T(1024)(128)(2,1)S(1)} fusion(bf16[1152]{0:T(1024)(128)(2,1)S(1)} %reshape.140, s32[1024]{0:T(1024)S(1)} %broadcast_clamp_fusion), kind=kCustom, calls=%fused_computation | custom fusion | bytes 8192 | tf_op jit(solution)/shard_map/jit(_take)/gather | solution.py:128
  475.5 4.9 reshape.138
  480.4 2.1 convolution_convert_fusion.3
  482.5 9.8 %all_gather.7 = bf16[128,3584]{1,0:T(8,128)(2,1)S(1)} all-gather(bf16[128,896]{1,0:T(8,128)(2,1)S(1)} %convolution_convert_fusion.3), channel_id=1, replica_groups=mesh['zlo'=2,'core'=2,'expert'=64] {'zlo','core'}, dimensions={1}, use_global_device_ids=true | all-gather | bytes 1146880 | tf_op jit(solution)/shard_map/all_gather | solution.py:126
  (53 shorter events, 10.5 us)
Async XLA Ops:
  7.2 289.0 %copy-start = (bf16[1,3584,256]{2,1,0:T(8,128)(2,1)S(1)}, bf16[1,3584,256]{2,1,0:T(8,128)(2,1)}, u32[]{:S(2)}) copy-start(bf16[1,3584,256]{2,1,0:T(8,128)(2,1)} %param.10) | copy-start | bytes 5505028
  7.2 289.0 %all-gather.2.cloned.1.call-start = ((), (), s32[]{:S(2)}) async-start(), calls=%async_computation.4 | async-start | bytes 24772608 | tf_op jit(solution)/shard_map/all_gather | solution.py:91
  296.2 5.8 %copy-start.4 = (bf16[256,2,1792]{2,1,0:T(2,128)(2,1)S(1)}, bf16[256,2,1792]{2,1,0:T(2,128)(2,1)}, u32[]{:S(2)}) copy-start(bf16[256,2,1792]{2,1,0:T(2,128)(2,1)} %reshape_squeeze.12) | copy-start | bytes 5505028
  296.2 8.6 %copy-start.7 = (bf16[2,1152,3584]{2,1,0:T(8,128)(2,1)S(1)}, bf16[2,1152,3584]{2,1,0:T(8,128)(2,1)}, u32[]{:S(2)}) copy-start(bf16[2,1152,3584]{2,1,0:T(8,128)(2,1)} %all-gather.2.cloned.1.call-done) | copy-start | bytes 49545220
  304.8 3.1 copy-start.8
  314.8 2.6 copy-start.5
  328.5 3.2 copy-start.2
  386.9 2.0 copy-start.3
  398.6 16.1 %copy-start.9 = (f32[1152,256]{1,0:T(8,128)S(1)}, f32[1152,256]{1,0:T(8,128)}, u32[]{:S(2)}) copy-start(f32[1152,256]{1,0:T(8,128)} %copy-done.8) | copy-start | bytes 3538948
  402.0 64.8 %all-to-all-start.3 = ((bf16[64,127,128]{2,1,0:T(8,128)(2,1)}), bf16[64,127,128]{2,1,0:T(8,128)(2,1)}, u32[]{:S(2)}, u32[]{:S(2)}) async-start(bf16[64,127,128]{2,1,0:T(8,128)(2,1)} %fusion.23), calls=%async_computation.3 | async-start | bytes 4194304 | tf_op jit(solution)/shard_map/all_to_all | solution.py:120
  422.3 5.4 %copy-start.6 = (bf16[1152,256,1]{1,0,2:T(8,128)(2,1)S(1)}, bf16[1152,256,1]{1,0,2:T(8,128)(2,1)}, u32[]{:S(2)}) copy-start(bf16[1152,256,1]{1,0,2:T(8,128)(2,1)} %copy-done.5) | copy-start | bytes 1769476
  475.5 17.7 %copy-start.1 = (bf16[1,3584,256]{2,1,0:T(8,128)(2,1)S(1)}, bf16[1,3584,256]{2,1,0:T(8,128)(2,1)}, u32[]{:S(2)}) copy-start(bf16[1,3584,256]{2,1,0:T(8,128)(2,1)} %param.10) | copy-start | bytes 5505028
Sparse Core Ops, SparseCore 0:
  265.0 31.1 all-gather.1

commit v7 on v6

--- a/solution.py
+++ b/solution.py
@@ -86,9 +86,9 @@
     )
     recv = lax.all_to_all(packed, "expert", split_axis=0, concat_axis=0, tiled=True)
     rows = experts * capacity
-    recv_xu = recv[:, :body, :].reshape(rows, 2 * half)
     recv_p = recv[:, body, :capacity].reshape(rows)
-    all_xu = lax.all_gather(recv_xu, "core", axis=0, tiled=False)
+    all_xu = lax.all_gather(recv[:, :body, :], "core", axis=0, tiled=False)
+    all_xu = all_xu.reshape(n_c, rows, 2 * half)
     all_x = all_xu[..., :half]
     all_u = all_xu[..., half:]
     row_grad, score, grad_in, grad_out = expert_terms(

time: 502 us -> 513 us (1.022)
  local copies, waits for them, and re-layouts: 79 us -> 93.2 us
    reshape x0 -> x1, local copies, waits for them, and re-layouts: none -> 29.7 us  [per_device(): all_xu = all_xu.reshape(n_c, rows, 2 * half)]
    another operation x1 -> x0, local copies, waits for them, and re-layouts: 15.5 us -> none  [per_device(): all_xu = lax.all_gather(recv_xu, 'core', axis=0, tiled=False)]
where the time goes in v7:
time: 513 us; the launch traced here: 511 us
  blocking collectives  273 us (53%)
  local copies, waits for them, and re-layouts  93.2 us (18%)
  waiting for transfers between devices  57.9 us (11%)
  matrix products  37.8 us (7%)
  other arithmetic  21.9 us (4%)
  between operations  14.3 us (3%)
  starting transfers between devices  12.7 us (2%)
    all_to_all x1, blocking collectives, per_device(): lax.all_to_all(packed, 'expert', split_axis=0, concat_axis=0, tiled=True)  203 us
    all_to_all x1, blocking collectives, per_device(): lax.all_to_all(chunk2, 'zlo', split_axis=0, concat_axis=0, tiled=True)  50.5 us
    all_to_all x1, waiting for transfers between devices, per_device(): lax.all_to_all(packed2, 'expert', split_axis=0, concat_axis=0, tiled=True)  32.6 us
    reshape x1, local copies, waits for them, and re-layouts, per_device(): all_xu = all_xu.reshape(n_c, rows, 2 * half)  29.7 us
    all_gather x1, waiting for transfers between devices, per_device(): all_xu = lax.all_gather(recv[:, :body, :], 'core', axis=0, tiled=False)  25.3 us
    reshape x1, local copies, waits for them, and re-layouts, per_device(): slot_xu.reshape(experts, body, 128)  16.1 us
    unnamed x26, local copies, waits for them, and re-layouts  13.8 us
    all_to_all x1, starting transfers between devices, per_device(): lax.all_to_all(packed2, 'expert', split_axis=0, concat_axis=0, tiled=True)  12.6 us
  transfers between devices with their start and end apart: 2, of which 2 were waited for; matrix products, arithmetic and copies ran while one was open for 5% of the time, Pallas kernels for 0%

profile of v7, /device:TPU:1, one launch (start us, length us, event | category | flops | bytes accessed | tf_op | source)
XLA Modules:
  0.0 510.6 jit_solution(16295491619694328350)
XLA Ops:
  10.9 1.5 convert_reduce_fusion
  13.6 5.5 %convolution_convert_fusion = bf16[1152,3584]{1,0:T(8,128)(2,1)} fusion(bf16[128,1792]{1,0:T(8,128)(2,1)S(1)} %get-tuple-element.26, bf16[128,1792]{1,0:T(8,128)(2,1)S(1)} %get-tuple-element.27, bf16[128,1152]{1,0:T(8,128)(2,1)S(1)} %convert_reduce_fusion), kind=kOutput, calls=%fused_computation.7 | convolution fusion | flops 1062928384 | bytes 9469952 | tf_op jit(solution)/shard_map/dot_general | solution.py:73
  19.2 16.1 %reshape.133 = bf16[64,504,128]{2,1,0:T(8,128)(2,1)} reshape(bf16[1152,3584]{1,0:T(8,128)(2,1)} %convolution_convert_fusion) | data formatting | bytes 16515072 | tf_op jit(solution)/shard_map/reshape | solution.py:82
  35.3 4.4 fusion.3
  39.7 202.6 %all_to_all.20 = bf16[64,505,128]{2,1,0:T(8,128)(2,1)} all-to-all(bf16[64,505,128]{2,1,0:T(8,128)(2,1)S(1)} %fusion.3), channel_id=1, replica_groups=mesh['zlo'=2,'core'=2,'expert'=64] {'expert'}, dimensions={0} | all-to-all | bytes 16547840 | tf_op jit(solution)/shard_map/all_to_all | solution.py:87
  242.4 7.1 %slice.46 = bf16[64,504,128]{2,1,0:T(8,128)(2,1)} slice(bf16[64,505,128]{2,1,0:T(8,128)(2,1)} %all_to_all.20), slice={[0:64], [0:504], [0:128]} | slice | bytes 16515072 | tf_op jit(solution)/shard_map/slice | solution.py:90
  249.5 4.9 reshape_squeeze.12
  255.5 25.3 %all-gather.3.cloned.1.call-done = bf16[128,504,128]{2,1,0:T(8,128)(2,1)} async-done(((bf16[64,504,128]{2,1,0:T(8,128)(2,1)}), bf16[128,504,128]{2,1,0:T(8,128)(2,1)}) %all-gather.3.cloned.1.call-update) | async-done | bytes 16515088 | tf_op jit(solution)/shard_map/all_gather | solution.py:90
  280.8 29.7 %reshape.136 = bf16[2,1152,3584]{2,1,0:T(8,128)(2,1)} reshape(bf16[128,504,128]{2,1,0:T(8,128)(2,1)} %all-gather.3.cloned.1.call-done) | data formatting | bytes 33030144 | tf_op jit(solution)/shard_map/reshape | solution.py:91
  310.5 5.8 %fusion.14 = f32[1152,256]{1,0:T(8,128)S(1)} fusion(bf16[2,1792,256]{2,1,0:T(8,128)(2,1)S(1)} %bitcast.39, bf16[2,1152,3584]{2,1,0:T(8,128)(2,1)} %reshape.136), kind=kOutput, calls=%fused_computation.28 | convolution fusion | flops 2113929216 | bytes 11272192 | tf_op jit(solution)/shard_map/hrk,hkf->rf/dot_general | solution.py:33
  316.3 2.2 copy-done.4
  319.0 3.1 fusion.2
  322.1 2.5 fusion.19
  324.8 2.6 convolution_convert_fusion.1
  328.2 10.3 %all_to_all.21 = bf16[2,2,1168,896]{3,2,0,1:T(8,128)(2,1)S(1)} all-to-all(bf16[2,2,1168,896]{3,2,0,1:T(8,128)(2,1)S(1)} %pad_maximum_fusion), channel_id=1, replica_groups=mesh['zlo'=2,'core'=2,'expert'=64] {'core'}, dimensions={1} | all-to-all | bytes 16744448 | tf_op jit(solution)/shard_map/all_to_all | solution.py:101
  338.4 3.2 copy-done.2
  341.7 4.5 slice_reduce_fusion
  346.6 50.5 %all_to_all.22 = bf16[2,1184,896]{2,1,0:T(8,128)(2,1)S(1)} all-to-all(bf16[2,1184,896]{2,1,0:T(8,128)(2,1)S(1)} %pad_maximum_fusion.1), channel_id=1, replica_groups=mesh['zlo'=2,'core'=2,'expert'=64] {'zlo'}, dimensions={0} | all-to-all | bytes 8486912 | tf_op jit(solution)/shard_map/all_to_all | solution.py:105
  397.1 2.0 copy-done.3
  399.3 4.9 slice_reduce_fusion.1
  404.1 4.7 reshape.139
  408.8 3.4 fusion.23
  412.2 12.6 %all-to-all-start.3 = ((bf16[64,127,128]{2,1,0:T(8,128)(2,1)}), bf16[64,127,128]{2,1,0:T(8,128)(2,1)}, u32[]{:S(2)}, u32[]{:S(2)}) async-start(bf16[64,127,128]{2,1,0:T(8,128)(2,1)} %fusion.23), calls=%async_computation.3 | async-start | bytes 4194304 | tf_op jit(solution)/shard_map/all_to_all | solution.py:120
  425.0 7.5 %convolution_convert_fusion.2 = bf16[256,2,1792]{2,0,1:T(8,128)(2,1)} fusion(f32[1152]{0:T(1024)S(1)} %reshape.143, bf16[2,1152,3584]{2,1,0:T(8,128)(2,1)} %reshape.136, f32[1152,256]{1,0:T(8,128)S(1)} %copy-done.9), kind=kOutput, calls=%fused_computation.27 | convolution fusion | flops 2128707584 | bytes 11276800 | tf_op jit(solution)/shard_map/rf,hrk->fhk/dot_general | solution.py:43
  432.5 2.9 copy.80
  435.3 2.6 copy.82
  437.9 7.2 %fusion.11 = bf16[2,1792,256]{2,1,0:T(8,128)(2,1)} fusion(bf16[1152,256,1]{1,0,2:T(8,128)(2,1)S(1)} %copy-done.7, bf16[2,1152,3584]{2,1,0:T(8,128)(2,1)} %reshape.136), kind=kOutput, calls=%fused_computation.26 | convolution fusion | flops 2114846720 | bytes 10682368 | tf_op jit(solution)/shard_map/hrk,rf->hkf/dot_general | solution.py:44
  445.1 32.6 %all-to-all-done.3 = bf16[64,127,128]{2,1,0:T(8,128)(2,1)} async-done(((bf16[64,127,128]{2,1,0:T(8,128)(2,1)}), bf16[64,127,128]{2,1,0:T(8,128)(2,1)}, u32[]{:S(2)}, u32[]{:S(2)}) %all-to-all-start.3) | async-done | bytes 2080800 | tf_op jit(solution)/shard_map/all_to_all | solution.py:120
  478.9 6.8 %gather_fusion = bf16[1024]{0:T(1024)(128)(2,1)S(1)} fusion(bf16[1152]{0:T(1024)(128)(2,1)S(1)} %reshape.144, s32[1024]{0:T(1024)S(1)} %broadcast_clamp_fusion), kind=kCustom, calls=%fused_computation | custom fusion | bytes 8192 | tf_op jit(solution)/shard_map/jit(_take)/gather | solution.py:128
  486.4 4.9 reshape.142
  491.3 2.1 convolution_convert_fusion.3
  493.4 9.4 %all_gather.11 = bf16[128,3584]{1,0:T(8,128)(2,1)S(1)} all-gather(bf16[128,896]{1,0:T(8,128)(2,1)S(1)} %convolution_convert_fusion.3), channel_id=1, replica_groups=mesh['zlo'=2,'core'=2,'expert'=64] {'zlo','core'}, dimensions={1}, use_global_device_ids=true | all-gather | bytes 1146880 | tf_op jit(solution)/shard_map/all_gather | solution.py:126
  (53 shorter events, 11.0 us)
Async XLA Ops:
  7.2 303.3 %copy-start = (bf16[1,3584,256]{2,1,0:T(8,128)(2,1)S(1)}, bf16[1,3584,256]{2,1,0:T(8,128)(2,1)}, u32[]{:S(2)}) copy-start(bf16[1,3584,256]{2,1,0:T(8,128)(2,1)} %param.10) | copy-start | bytes 5505028
  7.2 273.6 %all-gather.3.cloned.1.call-start = ((), (), s32[]{:S(2)}) async-start(), calls=%async_computation.4 | async-start | bytes 24772608 | tf_op jit(solution)/shard_map/all_gather | solution.py:90
  310.5 8.0 %copy-start.4 = (bf16[2,1152,3584]{2,1,0:T(8,128)(2,1)S(1)}, bf16[2,1152,3584]{2,1,0:T(8,128)(2,1)}, u32[]{:S(2)}) copy-start(bf16[2,1152,3584]{2,1,0:T(8,128)(2,1)} %reshape.136) | copy-start | bytes 49545220
  310.5 8.5 %copy-start.5 = (bf16[256,2,1792]{2,1,0:T(2,128)(2,1)S(1)}, bf16[256,2,1792]{2,1,0:T(2,128)(2,1)}, u32[]{:S(2)}) copy-start(bf16[256,2,1792]{2,1,0:T(2,128)(2,1)} %reshape_squeeze.12) | copy-start | bytes 5505028
  319.0 3.1 copy-start.8
  324.7 2.7 copy-start.6
  338.4 3.2 copy-start.2
  397.1 2.0 copy-start.3
  408.8 16.2 %copy-start.9 = (f32[1152,256]{1,0:T(8,128)S(1)}, f32[1152,256]{1,0:T(8,128)}, u32[]{:S(2)}) copy-start(f32[1152,256]{1,0:T(8,128)} %copy-done.8) | copy-start | bytes 3538948
  412.2 65.5 %all-to-all-start.3 = ((bf16[64,127,128]{2,1,0:T(8,128)(2,1)}), bf16[64,127,128]{2,1,0:T(8,128)(2,1)}, u32[]{:S(2)}, u32[]{:S(2)}) async-start(bf16[64,127,128]{2,1,0:T(8,128)(2,1)} %fusion.23), calls=%async_computation.3 | async-start | bytes 4194304 | tf_op jit(solution)/shard_map/all_to_all | solution.py:120
  432.5 5.4 %copy-start.7 = (bf16[1152,256,1]{1,0,2:T(8,128)(2,1)S(1)}, bf16[1152,256,1]{1,0,2:T(8,128)(2,1)}, u32[]{:S(2)}) copy-start(bf16[1152,256,1]{1,0,2:T(8,128)(2,1)} %copy-done.6) | copy-start | bytes 1769476
  486.4 17.3 %copy-start.1 = (bf16[1,3584,256]{2,1,0:T(8,128)(2,1)S(1)}, bf16[1,3584,256]{2,1,0:T(8,128)(2,1)}, u32[]{:S(2)}) copy-start(bf16[1,3584,256]{2,1,0:T(8,128)(2,1)} %param.10) | copy-start | bytes 5505028
Sparse Core Ops, SparseCore 0:
  249.6 31.1 all-gather.2

commit v8 on v6

--- a/solution.py
+++ b/solution.py
@@ -125,7 +125,9 @@
     )
     grad_tokens = lax.all_gather(token_part.astype(jnp.bfloat16), DP, axis=1, tiled=True)
     gate_grad = (
-        jnp.take(back_s.reshape(-1).astype(jnp.float32), target).reshape(count, top)
+        jnp.dot(
+            placing.astype(jnp.bfloat16), back_s.reshape(-1), preferred_element_type=jnp.float32
+        ).reshape(count, top)
     ).astype(jnp.bfloat16)
     grad_w_in = grad_in.astype(jnp.bfloat16)[None]
     grad_w_out = grad_out.astype(jnp.bfloat16)[None]

time: 502 us -> 502 us (level)
  matrix products: 42 us -> 47.9 us
  local copies, waits for them, and re-layouts: 79 us -> 73.2 us
    gather x2 -> x0, local copies, waits for them, and re-layouts: 6.89 us -> none  [per_device(): jnp.take(back_s.reshape(-1).astype(jnp.float32), target).reshape(count, top)]
    dot_general x0 -> x1, matrix products: none -> 5.92 us  [per_device(): jnp.dot(placing.astype(jnp.bfloat16), back_s.reshape(-1), preferred_eleme...]
    unnamed x26 -> x25, local copies, waits for them, and re-layouts: 13.9 us -> 13.2 us
where the time goes in v8:
time: 502 us; the launch traced here: 500 us
  blocking collectives  272 us (54%)
  local copies, waits for them, and re-layouts  73.2 us (15%)
  waiting for transfers between devices  58 us (12%)
  matrix products  47.9 us (10%)
  other arithmetic  21.5 us (4%)
  between operations  14.3 us (3%)
  starting transfers between devices  12.6 us (3%)
    all_to_all x1, blocking collectives, per_device(): lax.all_to_all(packed, 'expert', split_axis=0, concat_axis=0, tiled=True)  202 us
    all_to_all x1, blocking collectives, per_device(): lax.all_to_all(chunk2, 'zlo', split_axis=0, concat_axis=0, tiled=True)  50.3 us
    all_to_all x1, waiting for transfers between devices, per_device(): lax.all_to_all(packed2, 'expert', split_axis=0, concat_axis=0, tiled=True)  32 us
    all_gather x1, waiting for transfers between devices, per_device(): all_xu = lax.all_gather(recv_xu, 'core', axis=0, tiled=False)  25.9 us
    reshape x1, local copies, waits for them, and re-layouts, per_device(): slot_xu.reshape(experts, body, 128)  16.1 us
    another operation x1, local copies, waits for them, and re-layouts, per_device(): all_xu = lax.all_gather(recv_xu, 'core', axis=0, tiled=False)  15.5 us
    unnamed x25, local copies, waits for them, and re-layouts  13.2 us
    all_to_all x1, starting transfers between devices, per_device(): lax.all_to_all(packed2, 'expert', split_axis=0, concat_axis=0, tiled=True)  12.6 us
  transfers between devices with their start and end apart: 2, of which 2 were waited for; matrix products, arithmetic and copies ran while one was open for 5% of the time, Pallas kernels for 0%

profile of v8, /device:TPU:1, one launch (start us, length us, event | category | flops | bytes accessed | tf_op | source)
XLA Modules:
  0.0 499.9 jit_solution(15631099759143193364)
XLA Ops:
  11.8 1.5 convert_reduce_fusion
  14.5 5.5 %convolution_convert_fusion = bf16[1152,3584]{1,0:T(8,128)(2,1)} fusion(bf16[128,1792]{1,0:T(8,128)(2,1)S(1)} %get-tuple-element.24, bf16[128,1792]{1,0:T(8,128)(2,1)S(1)} %get-tuple-element.25, bf16[128,1152]{1,0:T(8,128)(2,1)S(1)} %convert_reduce_fusion), kind=kOutput, calls=%fused_computation.6 | convolution fusion | flops 1062928384 | bytes 9469952 | tf_op jit(solution)/shard_map/dot_general | solution.py:73
  20.0 16.1 %reshape.120 = bf16[64,504,128]{2,1,0:T(8,128)(2,1)} reshape(bf16[1152,3584]{1,0:T(8,128)(2,1)} %convolution_convert_fusion) | data formatting | bytes 16515072 | tf_op jit(solution)/shard_map/reshape | solution.py:82
  36.1 4.4 fusion.3
  40.6 202.0 %all_to_all.20 = bf16[64,505,128]{2,1,0:T(8,128)(2,1)} all-to-all(bf16[64,505,128]{2,1,0:T(8,128)(2,1)S(1)} %fusion.3), channel_id=1, replica_groups=mesh['zlo'=2,'core'=2,'expert'=64] {'expert'}, dimensions={0} | all-to-all | bytes 16547840 | tf_op jit(solution)/shard_map/all_to_all | solution.py:87
  242.5 7.1 %slice.44 = bf16[64,504,128]{2,1,0:T(8,128)(2,1)} slice(bf16[64,505,128]{2,1,0:T(8,128)(2,1)} %all_to_all.20), slice={[0:64], [0:504], [0:128]} | slice | bytes 16515072 | tf_op jit(solution)/shard_map/slice | solution.py:89
  249.6 15.5 %all_gather_reshape.3 = bf16[1,1152,3584]{2,1,0:T(8,128)(2,1)} reshape(bf16[64,504,128]{2,1,0:T(8,128)(2,1)} %slice.44) | data formatting | bytes 16515072 | tf_op jit(solution)/shard_map/all_gather;reshape | solution.py:91
  265.1 4.9 reshape_squeeze.14
  271.1 25.9 %all-gather.2.cloned.1.call-done = bf16[2,1152,3584]{2,1,0:T(8,128)(2,1)} async-done(((bf16[1,1152,3584]{2,1,0:T(8,128)(2,1)}), bf16[2,1152,3584]{2,1,0:T(8,128)(2,1)}) %all-gather.2.cloned.1.call-update) | async-done | bytes 16515088 | tf_op jit(solution)/shard_map/all_gather | solution.py:91
  297.1 5.8 %fusion.14 = f32[1152,256]{1,0:T(8,128)S(1)} fusion(bf16[2,1792,256]{2,1,0:T(8,128)(2,1)S(1)} %bitcast.44, bf16[2,1152,3584]{2,1,0:T(8,128)(2,1)} %all-gather.2.cloned.1.call-done), kind=kOutput, calls=%fused_computation.29 | convolution fusion | flops 2113929216 | bytes 11272192 | tf_op jit(solution)/shard_map/hrk,hkf->rf/dot_general | solution.py:33
  302.9 2.8 copy-done.7
  305.7 3.1 fusion.2
  308.8 6.8 %fusion.19 = bf16[1152,256,1]{1,0,2:T(8,128)(2,1)S(1)} fusion(f32[1152]{0:T(1024)S(1)} %reshape.129, bf16[2,1152,3584]{2,1,0:T(8,128)(2,1)} %all-gather.2.cloned.1.call-done, bf16[256,2,1792]{2,1,0:T(2,128)(2,1)} %reshape_squeeze.14, f32[1152,256]{1,0:T(8,128)} %copy-done.8), kind=kOutput, calls=%fused_computation.33 | convolution fusion | flops 2128969728 | bytes 11866624 | tf_op jit(solution)/shard_map/hrk,fhk->rf/dot_general | solution.py:40
  315.6 2.6 convolution_convert_fusion.1
  319.0 10.3 %all_to_all.21 = bf16[2,2,1168,896]{3,2,0,1:T(8,128)(2,1)S(1)} all-to-all(bf16[2,2,1168,896]{3,2,0,1:T(8,128)(2,1)S(1)} %pad_maximum_fusion), channel_id=1, replica_groups=mesh['zlo'=2,'core'=2,'expert'=64] {'core'}, dimensions={1} | all-to-all | bytes 16744448 | tf_op jit(solution)/shard_map/all_to_all | solution.py:101
  329.3 3.2 copy-done.2
  332.6 4.5 slice_reduce_fusion
  337.5 50.3 %all_to_all.22 = bf16[2,1184,896]{2,1,0:T(8,128)(2,1)S(1)} all-to-all(bf16[2,1184,896]{2,1,0:T(8,128)(2,1)S(1)} %pad_maximum_fusion.1), channel_id=1, replica_groups=mesh['zlo'=2,'core'=2,'expert'=64] {'zlo'}, dimensions={0} | all-to-all | bytes 8486912 | tf_op jit(solution)/shard_map/all_to_all | solution.py:105
  387.7 2.0 copy-done.3
  390.0 4.9 slice_reduce_fusion.1
  394.8 4.7 reshape.125
  399.5 3.4 fusion.27
  402.9 12.6 %all-to-all-start.3 = ((bf16[64,127,128]{2,1,0:T(8,128)(2,1)}), bf16[64,127,128]{2,1,0:T(8,128)(2,1)}, u32[]{:S(2)}, u32[]{:S(2)}) async-start(bf16[64,127,128]{2,1,0:T(8,128)(2,1)} %fusion.27), calls=%async_computation.3 | async-start | bytes 4194304 | tf_op jit(solution)/shard_map/all_to_all | solution.py:120
  415.5 7.5 %convolution_convert_fusion.2 = bf16[256,2,1792]{2,0,1:T(8,128)(2,1)} fusion(f32[1152]{0:T(1024)S(1)} %reshape.129, bf16[2,1152,3584]{2,1,0:T(8,128)(2,1)} %all-gather.2.cloned.1.call-done, f32[1152,256]{1,0:T(8,128)S(1)} %copy-done.9), kind=kOutput, calls=%fused_computation.28 | convolution fusion | flops 2128707584 | bytes 11276800 | tf_op jit(solution)/shard_map/rf,hrk->fhk/dot_general | solution.py:43
  423.0 2.9 copy.83
  425.9 2.6 copy.84
  428.4 7.2 %fusion.11 = bf16[2,1792,256]{2,1,0:T(8,128)(2,1)} fusion(bf16[1152,256,1]{1,0,2:T(8,128)(2,1)S(1)} %copy-done.6, bf16[2,1152,3584]{2,1,0:T(8,128)(2,1)} %all-gather.2.cloned.1.call-done), kind=kOutput, calls=%fused_computation.27 | convolution fusion | flops 2114846720 | bytes 10682368 | tf_op jit(solution)/shard_map/hrk,rf->hkf/dot_general | solution.py:44
  435.6 32.0 %all-to-all-done.3 = bf16[64,127,128]{2,1,0:T(8,128)(2,1)} async-done(((bf16[64,127,128]{2,1,0:T(8,128)(2,1)}), bf16[64,127,128]{2,1,0:T(8,128)(2,1)}, u32[]{:S(2)}, u32[]{:S(2)}) %all-to-all-start.3) | async-done | bytes 2080800 | tf_op jit(solution)/shard_map/all_to_all | solution.py:120
  468.8 5.9 %fusion.23 = bf16[1,128,8]{2,0,1:T(2,128)(2,1)S(1)} fusion(bf16[1152,1,1]{0,1,2:T(2,128)(2,1)S(1)} %reshape.136, s32[128,8]{1,0:T(8,128)S(1)} %copy.72), kind=kOutput, calls=%fused_computation.35 | convolution fusion | flops 5898240 | bytes 8448 | tf_op jit(solution)/shard_map/dot_general | solution.py:128
  475.4 4.9 reshape.128
  480.2 2.1 convolution_convert_fusion.3
  482.3 9.8 %all_gather.7 = bf16[128,3584]{1,0:T(8,128)(2,1)S(1)} all-gather(bf16[128,896]{1,0:T(8,128)(2,1)S(1)} %convolution_convert_fusion.3), channel_id=1, replica_groups=mesh['zlo'=2,'core'=2,'expert'=64] {'zlo','core'}, dimensions={1}, use_global_device_ids=true | all-gather | bytes 1146880 | tf_op jit(solution)/shard_map/all_gather | solution.py:126
  (50 shorter events, 11.2 us)
Async XLA Ops:
  7.2 289.9 %copy-start = (bf16[1,3584,256]{2,1,0:T(8,128)(2,1)S(1)}, bf16[1,3584,256]{2,1,0:T(8,128)(2,1)}, u32[]{:S(2)}) copy-start(bf16[1,3584,256]{2,1,0:T(8,128)(2,1)} %param.10) | copy-start | bytes 5505028
  7.2 289.9 %all-gather.2.cloned.1.call-start = ((), (), s32[]{:S(2)}) async-start(), calls=%async_computation.4 | async-start | bytes 24772608 | tf_op jit(solution)/shard_map/all_gather | solution.py:91
  297.1 5.8 %copy-start.4 = (bf16[256,2,1792]{2,1,0:T(2,128)(2,1)S(1)}, bf16[256,2,1792]{2,1,0:T(2,128)(2,1)}, u32[]{:S(2)}) copy-start(bf16[256,2,1792]{2,1,0:T(2,128)(2,1)} %reshape_squeeze.14) | copy-start | bytes 5505028
  297.1 8.6 %copy-start.7 = (bf16[2,1152,3584]{2,1,0:T(8,128)(2,1)S(1)}, bf16[2,1152,3584]{2,1,0:T(8,128)(2,1)}, u32[]{:S(2)}) copy-start(bf16[2,1152,3584]{2,1,0:T(8,128)(2,1)} %all-gather.2.cloned.1.call-done) | copy-start | bytes 49545220
  305.7 3.1 copy-start.8
  315.6 2.6 copy-start.5
  329.3 3.2 copy-start.2
  387.7 2.0 copy-start.3
  399.5 16.0 %copy-start.9 = (f32[1152,256]{1,0:T(8,128)S(1)}, f32[1152,256]{1,0:T(8,128)}, u32[]{:S(2)}) copy-start(f32[1152,256]{1,0:T(8,128)} %copy-done.8) | copy-start | bytes 3538948
  402.9 64.7 %all-to-all-start.3 = ((bf16[64,127,128]{2,1,0:T(8,128)(2,1)}), bf16[64,127,128]{2,1,0:T(8,128)(2,1)}, u32[]{:S(2)}, u32[]{:S(2)}) async-start(bf16[64,127,128]{2,1,0:T(8,128)(2,1)} %fusion.27), calls=%async_computation.3 | async-start | bytes 4194304 | tf_op jit(solution)/shard_map/all_to_all | solution.py:120
  423.0 5.4 %copy-start.6 = (bf16[1152,256,1]{1,0,2:T(8,128)(2,1)S(1)}, bf16[1152,256,1]{1,0,2:T(8,128)(2,1)}, u32[]{:S(2)}) copy-start(bf16[1152,256,1]{1,0,2:T(8,128)(2,1)} %copy-done.5) | copy-start | bytes 1769476
  475.4 17.7 %copy-start.1 = (bf16[1,3584,256]{2,1,0:T(8,128)(2,1)S(1)}, bf16[1,3584,256]{2,1,0:T(8,128)(2,1)}, u32[]{:S(2)}) copy-start(bf16[1,3584,256]{2,1,0:T(8,128)(2,1)} %param.10) | copy-start | bytes 5505028
Sparse Core Ops, SparseCore 0:
  265.2 31.8 all-gather.1
